TPU v7x, 256 devices: a whole 4x4x8 slice. The times are simulated.
256 devices in a mesh: dp: 4 (over x), expert: 64 (over y, z, core).
Axes of the slice: x: 4, y: 4, z: 8, core: 2. Of those that a mesh axis runs over, the one named last changes fastest.
Arguments:
- features: bfloat16 [65536, 512], P(('dp', 'expert')), may hold values from -6 to 6
- slots: int32 [65536], P(('dp', 'expert')), may hold values from 0 to 31
- routes: int32 [65536, 2], P(('dp', 'expert')), may hold values from 0 to 63, all different within a row; in each aligned block of 256 rows (0 to 255, 256 to 511, ...) at most 16 rows name the same one
- cotangent: bfloat16 [65536, 512], P(('dp', 'expert')), may hold values from -1.5 to 1.5
- pos_table: bfloat16 [32, 64], replicated, may hold values from -6 to 6
- tower_in: bfloat16 [64, 256], replicated, may hold values from -0.75 to 0.75
- tower_out: bfloat16 [256, 512], replicated, may hold values from -0.375 to 0.375
- router: bfloat16 [512, 64], replicated, may hold values from -0.5 to 0.5
- w_up: bfloat16 [64, 512, 2048], P('expert'), may hold values from -0.25 to 0.25
- w_down: bfloat16 [64, 2048, 512], P('expert'), may hold values from -0.125 to 0.125
Outputs:
- layer_out: bfloat16 [65536, 512], P(('dp', 'expert'))
- grad_in: bfloat16 [65536, 512], P(('dp', 'expert'))
- grad_up: bfloat16 [64, 512, 2048], P('expert')
- grad_down: bfloat16 [64, 2048, 512], P('expert')
Inputs may be any that keep to these rules, and one draw needn't show every extreme that they name: `routes`: within the rows of one device no expert is named by more than 16 rows; in some devices' rows one expert is named by exactly 16.
All inputs are finite; a program needn't handle non-finite values.
Results may differ from a plain program's by a relative error of at most 0.013.
Values may be sent and summed in bfloat16 or wider, within the bound.
No kernel may reach another device: no remote copies, remote signals or barrier semaphores. Data moves between devices by JAX's collectives and lax.ppermute only.
A program may use at most 128 MiB of HBM per device.

v0:
```python
import jax
import jax.numpy as jnp
from jax import lax
from jax.sharding import PartitionSpec as P

TOP = 2


coef_a = 0.7978845608028654
coef_b = 0.044715


def gelu_pair(pre_act):
    inner = coef_a * (pre_act + coef_b * pre_act * pre_act * pre_act)
    tanh_val = jnp.tanh(inner)
    activated = 0.5 * pre_act * (1.0 + tanh_val)
    gelu_slope = 0.5 * (1.0 + tanh_val) + 0.5 * pre_act * (1.0 - tanh_val * tanh_val) * coef_a * (
        1.0 + 3.0 * coef_b * pre_act * pre_act
    )
    return (activated, gelu_slope)


def contract_rows(left, right):
    return lax.dot_general(
        left, right, (((0,), (0,)), ((), ())), preferred_element_type=jnp.float32
    )


def contract_cols(left, right):
    return lax.dot_general(
        left, right, (((1,), (1,)), ((), ())), preferred_element_type=jnp.float32
    )


def expert_forward(flat_in, w_up_one, w_down_one):
    pre_act = jnp.dot(flat_in, w_up_one, preferred_element_type=jnp.float32)
    activated, gelu_slope = gelu_pair(pre_act)
    hidden = activated.astype(jnp.bfloat16)
    outputs = jnp.dot(hidden, w_down_one, preferred_element_type=jnp.float32).astype(jnp.bfloat16)
    return (hidden, gelu_slope, outputs)


def expert_backward(flat_in, flat_cot, hidden, gelu_slope, w_up_one, w_down_one):
    grad_down_part = contract_rows(hidden, flat_cot)
    d_hidden = contract_cols(flat_cot, w_down_one)
    d_pre = (d_hidden * gelu_slope).astype(jnp.bfloat16)
    d_inputs = contract_cols(d_pre, w_up_one).astype(jnp.bfloat16)
    grad_up_part = contract_rows(flat_in, d_pre)
    sum_up, sum_down = (
        lax.psum(grad_up_part.astype(jnp.bfloat16), "dp").astype(jnp.float32),
        lax.psum(grad_down_part.astype(jnp.bfloat16), "dp").astype(jnp.float32),
    )
    return (d_inputs, sum_up, sum_down)


def per_device(
    features, slots, routes, cotangent, pos_table, tower_in, tower_out, router, w_up, w_down
):
    tok_rows = features.shape[0]
    feature_width = features.shape[1]
    n_experts = router.shape[1]
    capacity = 2 * TOP * tok_rows // n_experts
    pos_hidden = jax.nn.relu(jnp.dot(pos_table, tower_in, preferred_element_type=jnp.float32))
    pos_rows = jnp.dot(pos_hidden, tower_out.astype(jnp.float32), precision=lax.Precision.HIGHEST)
    slot_hot = (slots[:, None] == jnp.arange(pos_table.shape[0], dtype=jnp.int32)[None, :]).astype(
        jnp.float32
    )
    pos_feats = jnp.dot(slot_hot, pos_rows, precision=lax.Precision.HIGHEST)
    mixed_in = (features.astype(jnp.float32) + pos_feats).astype(jnp.bfloat16)
    logits = jnp.dot(mixed_in, router, preferred_element_type=jnp.float32)
    expert_ids = jnp.arange(n_experts, dtype=jnp.int32)
    route_hot = routes[:, :, None] == expert_ids[None, None, :]
    chosen = jnp.sum(jnp.where(route_hot, logits[:, None, :], 0.0), axis=2)
    squashed = 1.0 / (1.0 + jnp.exp(-chosen))
    gate_total = jnp.sum(squashed, axis=1, keepdims=True)
    gates = squashed / gate_total
    cot_wide = cotangent.astype(jnp.float32)
    slot_cot = (gates[:, :, None] * cot_wide[:, None, :]).astype(jnp.bfloat16)
    flat_routes = routes.reshape(-1)
    flat_hot = route_hot.reshape(-1, n_experts).astype(jnp.int32)
    before = jnp.cumsum(flat_hot, axis=0, dtype=jnp.int32) - flat_hot
    slot_rank = jnp.sum(before * flat_hot, axis=1, dtype=jnp.int32)
    slot_place = flat_routes * capacity + slot_rank
    buffer_shape = (n_experts, capacity, feature_width)
    send_in = (
        jnp.zeros((n_experts * capacity, feature_width), jnp.bfloat16)
        .at[slot_place]
        .set(jnp.repeat(mixed_in, TOP, axis=0))
        .reshape(buffer_shape)
    )
    send_cot = (
        jnp.zeros((n_experts * capacity, feature_width), jnp.bfloat16)
        .at[slot_place]
        .set(slot_cot.reshape(-1, feature_width))
        .reshape(buffer_shape)
    )
    w_up_one = w_up[0]
    w_down_one = w_down[0]
    recv_in = lax.all_to_all(send_in, "expert", split_axis=0, concat_axis=0, tiled=True)
    flat_in = recv_in.reshape(-1, feature_width)
    hidden, gelu_slope, outputs = expert_forward(flat_in, w_up_one, w_down_one)
    back_out = lax.all_to_all(
        outputs.reshape(buffer_shape), "expert", split_axis=0, concat_axis=0, tiled=True
    )
    recv_cot = lax.all_to_all(send_cot, "expert", split_axis=0, concat_axis=0, tiled=True)
    flat_cot = recv_cot.reshape(-1, feature_width)
    d_inputs, sum_up, sum_down = expert_backward(
        flat_in, flat_cot, hidden, gelu_slope, w_up_one, w_down_one
    )
    back_grad = lax.all_to_all(
        d_inputs.reshape(buffer_shape), "expert", split_axis=0, concat_axis=0, tiled=True
    )
    expert_out = back_out.reshape(-1, feature_width)[slot_place].reshape(
        tok_rows, TOP, feature_width
    )
    slot_grad = back_grad.reshape(-1, feature_width)[slot_place].reshape(
        tok_rows, TOP, feature_width
    )
    expert_wide = expert_out.astype(jnp.float32)
    layer_out = (
        mixed_in.astype(jnp.float32) + jnp.sum(gates[:, :, None] * expert_wide, axis=1)
    ).astype(jnp.bfloat16)
    d_gates = jnp.sum(expert_wide * cot_wide[:, None, :], axis=2)
    mean_term = jnp.sum(gates * d_gates, axis=1, keepdims=True)
    d_chosen = (d_gates - mean_term) / gate_total * squashed * (1.0 - squashed)
    d_logits = jnp.sum(jnp.where(route_hot, d_chosen[:, :, None], 0.0), axis=1)
    d_router = lax.dot_general(
        d_logits,
        router.astype(jnp.float32),
        (((1,), (1,)), ((), ())),
        precision=lax.Precision.HIGHEST,
    )
    grad_in = (cot_wide + jnp.sum(slot_grad.astype(jnp.float32), axis=1) + d_router).astype(
        jnp.bfloat16
    )
    return (
        layer_out,
        grad_in,
        sum_up.astype(jnp.bfloat16)[None],
        sum_down.astype(jnp.bfloat16)[None],
    )


def solution(mesh):
    return jax.shard_map(
        per_device,
        mesh=mesh,
        in_specs=(
            P(("dp", "expert"), None),
            P(("dp", "expert")),
            P(("dp", "expert"), None),
            P(("dp", "expert"), None),
            P(),
            P(),
            P(),
            P(),
            P("expert", None, None),
            P("expert", None, None),
        ),
        out_specs=(
            P(("dp", "expert"), None),
            P(("dp", "expert"), None),
            P("expert", None, None),
            P("expert", None, None),
        ),
        check_vma=False,
    )
```

profile of v0, /device:TPU:1, one launch (start us, length us, event | category | flops | bytes accessed | tf_op | source)
XLA Modules:
  0.0 234.4 jit_solution(15027040676049464937)
XLA Ops:
  13.0 1.4 fusion.22
  15.0 3.5 %scatter_custom_fusion = bf16[1024,512]{1,0:T(8,128)(2,1)} fusion(s32[512]{0:T(512)S(1)} %bitcast.70, bf16[512,512]{1,0:T(8,128)(2,1)S(1)} %reshape.212, bf16[]{:T(256)} %constant.12.clone.1), kind=kCustom, calls=%fused_computation.39 | custom fusion | bytes 1048578 | tf_op jit(solution)/shard_map/scatter | solution.py:88
  18.5 13.3 %all-to-all-start = ((bf16[64,16,512]{2,1,0:T(8,128)(2,1)}), bf16[64,16,512]{2,1,0:T(8,128)(2,1)}, u32[]{:S(2)}, u32[]{:S(2)}) async-start(bf16[64,16,512]{2,1,0:T(8,128)(2,1)} %bitcast.3), calls=%async_computation | async-start | bytes 2097152 | tf_op jit(solution)/shard_map/all_to_all | solution.py:99
  35.7 1.7 mul.134
  37.4 4.3 %scatter_custom_fusion.1 = bf16[1024,512]{1,0:T(8,128)(2,1)} fusion(s32[512]{0:T(512)S(1)} %bitcast.71, f32[512,512]{1,0:T(8,128)} %mul.134, f32[512]{0:T(512)S(1)} %reshape.190, bf16[]{:T(256)} %constant.12.clone.1), kind=kCustom, calls=%fused_computation.35 | custom fusion | flops 524288 | bytes 2099202 | tf_op jit(solution)/shard_map/scatter | solution.py:94
  41.7 18.6 %all-to-all-done = bf16[64,16,512]{2,1,0:T(8,128)(2,1)} async-done(((bf16[64,16,512]{2,1,0:T(8,128)(2,1)}), bf16[64,16,512]{2,1,0:T(8,128)(2,1)}, u32[]{:S(2)}, u32[]{:S(2)}) %all-to-all-start) | async-done | bytes 1048608 | tf_op jit(solution)/shard_map/all_to_all | solution.py:99
  60.3 6.2 %all-to-all-start.2 = ((bf16[64,16,512]{2,1,0:T(8,128)(2,1)}), bf16[64,16,512]{2,1,0:T(8,128)(2,1)S(1)}, u32[]{:S(2)}, u32[]{:S(2)}) async-start(bf16[64,16,512]{2,1,0:T(8,128)(2,1)} %bitcast.9), calls=%async_computation.2 | async-start | bytes 2097152 | tf_op jit(solution)/shard_map/all_to_all | solution.py:105
  66.5 4.3 %fusion.14 = f32[1024,2048]{1,0:T(8,128)S(1)} fusion(bf16[1024,512]{1,0:T(8,128)(2,1)} %bitcast.4, bf16[1,512,2048]{2,1,0:T(8,128)(2,1)} %param.18), kind=kOutput, calls=%fused_computation.23 | convolution fusion | flops 2147483648 | bytes 11534336 | tf_op jit(solution)/shard_map/dot_general | solution.py:36
  70.8 3.2 %copy-done.6 = f32[1024,2048]{1,0:T(8,128)} copy-done((f32[1024,2048]{1,0:T(8,128)}, f32[1024,2048]{1,0:T(8,128)S(1)}, u32[]{:S(2)}) %copy-start.6) | copy-done | bytes 8388632
  74.0 4.0 %fusion.19 = bf16[1024,512]{1,0:T(8,128)(2,1)} fusion(bf16[1,2048,512]{2,1,0:T(8,128)(2,1)S(1)} %copy-done, f32[1024,2048]{1,0:T(8,128)S(1)} %fusion.14), kind=kOutput, calls=%fused_computation.26 | convolution fusion | flops 2166882304 | bytes 11534336 | tf_op jit(solution)/shard_map/dot_general | solution.py:39
  78.0 17.1 %all-to-all-done.2 = bf16[64,16,512]{2,1,0:T(8,128)(2,1)S(1)} async-done(((bf16[64,16,512]{2,1,0:T(8,128)(2,1)}), bf16[64,16,512]{2,1,0:T(8,128)(2,1)S(1)}, u32[]{:S(2)}, u32[]{:S(2)}) %all-to-all-start.2) | async-done | bytes 1048608 | tf_op jit(solution)/shard_map/all_to_all | solution.py:105
  96.0 6.2 %all-to-all-start.1 = ((bf16[64,16,512]{2,1,0:T(8,128)(2,1)}), bf16[64,16,512]{2,1,0:T(8,128)(2,1)S(1)}, u32[]{:S(2)}, u32[]{:S(2)}) async-start(bf16[64,16,512]{2,1,0:T(8,128)(2,1)} %bitcast.65), calls=%async_computation.1 | async-start | bytes 2097152 | tf_op jit(solution)/shard_map/all_to_all | solution.py:102
  102.2 8.8 %fusion.6 = bf16[1024,2048]{1,0:T(8,128)(2,1)S(1)} fusion(f32[1024,2048]{1,0:T(8,128)} %copy-done.6, bf16[1024,512]{1,0:T(8,128)(2,1)} %bitcast.67, bf16[1,2048,512]{2,1,0:T(8,128)(2,1)S(1)} %copy-done), kind=kOutput, calls=%fused_computation.12 | convolution fusion | flops 2187329536 | bytes 15728640 | tf_op jit(solution)/shard_map/dot_general | solution.py:30
  111.0 2.0 copy-done.8
  113.0 5.2 %fusion.7 = bf16[1,512,2048]{2,1,0:T(8,128)(2,1)} fusion(bf16[1024,512]{1,0:T(8,128)(2,1)} %bitcast.4, bf16[1024,2048]{1,0:T(8,128)(2,1)S(1)} %fusion.6), kind=kOutput, calls=%fused_computation.16 | convolution fusion | flops 2148532224 | bytes 7340032 | tf_op jit(solution)/shard_map/dot_general | solution.py:24
  118.2 4.3 %fusion.8 = bf16[1,2048,512]{2,1,0:T(8,128)(2,1)} fusion(bf16[1024,512]{1,0:T(8,128)(2,1)S(1)} %bitcast.68, f32[1024,2048]{1,0:T(8,128)S(1)} %copy-done.7), kind=kOutput, calls=%fused_computation.17 | convolution fusion | flops 2167406592 | bytes 11534336 | tf_op jit(solution)/shard_map/dot_general | solution.py:24
  122.5 6.2 %fusion.16 = bf16[1024,512]{1,0:T(8,128)(2,1)} fusion(bf16[1024,2048]{1,0:T(8,128)(2,1)} %copy-done.8, bf16[1,512,2048]{2,1,0:T(8,128)(2,1)} %param.18), kind=kOutput, calls=%fused_computation.25 | convolution fusion | flops 2148007936 | bytes 7340032 | tf_op jit(solution)/shard_map/dot_general | solution.py:30
  128.7 2.0 all-to-all-done.1
  130.7 8.5 %all-to-all-start.3 = ((bf16[64,16,512]{2,1,0:T(8,128)(2,1)}), bf16[64,16,512]{2,1,0:T(8,128)(2,1)}, u32[]{:S(2)}, u32[]{:S(2)}) async-start(bf16[64,16,512]{2,1,0:T(8,128)(2,1)} %bitcast.66), calls=%async_computation.3 | async-start | bytes 2097152 | tf_op jit(solution)/shard_map/all_to_all | solution.py:110
  139.3 1.8 convert_element_type.80
  141.8 2.6 %gather_fusion = bf16[512,512]{1,0:T(8,128)(2,1)} fusion(bf16[1024,512]{1,0:T(8,128)(2,1)S(1)} %bitcast.64, s32[1024]{0:T(1024)S(1)} %pad_clamp_fusion), kind=kCustom, calls=%fused_computation | custom fusion | bytes 1050624 | tf_op jit(solution)/shard_map/gather | solution.py:113
  144.4 1.7 reshape.188
  146.1 4.0 %multiply_reduce_fusion = (f32[256,2]{1,0:T(8,128)}, f32[256,512]{1,0:T(8,128)}) fusion(f32[256,2,512]{2,1,0:T(2,128)S(1)} %reshape.188, f32[256,512]{1,0:T(8,128)} %convert_element_type.80, f32[256,2]{1,0:T(8,128)S(1)} %copy.28), kind=kLoop, calls=%fused_computation.32 | loop fusion | flops 916992 | bytes 2101248 | tf_op jit(solution)/shard_map/reduce_sum | solution.py:123
  151.1 16.6 %all-to-all-done.3 = bf16[64,16,512]{2,1,0:T(8,128)(2,1)} async-done(((bf16[64,16,512]{2,1,0:T(8,128)(2,1)}), bf16[64,16,512]{2,1,0:T(8,128)(2,1)}, u32[]{:S(2)}, u32[]{:S(2)}) %all-to-all-start.3) | async-done | bytes 1048608 | tf_op jit(solution)/shard_map/all_to_all | solution.py:110
  167.7 4.0 %gather_fusion.1 = bf16[512,512]{1,0:T(8,128)(2,1)} fusion(bf16[1024,512]{1,0:T(8,128)(2,1)} %bitcast.12, s32[1024]{0:T(1024)S(1)} %pad_clamp_fusion), kind=kCustom, calls=%fused_computation.1 | custom fusion | bytes 1050624 | tf_op jit(solution)/shard_map/gather | solution.py:116
  171.7 1.7 reshape.191
  173.4 2.1 reduce_sum.79
  176.3 1.8 add_convert_fusion
  178.1 2.2 fusion.23
  180.4 41.0 %all-reduce.3.cloned.1.call-done = (bf16[1,512,2048]{2,1,0:T(8,128)(2,1)}, bf16[1,2048,512]{2,1,0:T(8,128)(2,1)}) async-done(((bf16[1,512,2048]{2,1,0:T(8,128)(2,1)}, bf16[1,2048,512]{2,1,0:T(8,128)(2,1)}), (bf16[1,512,2048]{2,1,0:T(8,128)(2,1)}, bf16[1,2048,512]{2,1,0:T(8,128)(2,1)})) %all-reduce.3.cloned.1.call-update) | async-done | bytes 4194320 | tf_op jit(solution)/shard_map/psum | solution.py:50
  221.3 3.2 %copy.40 = bf16[1,512,2048]{2,1,0:T(8,128)(2,1)} copy(bf16[1,512,2048]{2,1,0:T(8,128)(2,1)} %get-tuple-element.12) | data formatting | bytes 4194304
  224.5 3.0 %copy.41 = bf16[1,2048,512]{2,1,0:T(8,128)(2,1)} copy(bf16[1,2048,512]{2,1,0:T(8,128)(2,1)} %get-tuple-element.13) | data formatting | bytes 4194304
  (47 shorter events, 13.8 us)
Async XLA Ops:
  7.2 66.8 %copy-start = (bf16[1,2048,512]{2,1,0:T(8,128)(2,1)S(1)}, bf16[1,2048,512]{2,1,0:T(8,128)(2,1)}, u32[]{:S(2)}) copy-start(bf16[1,2048,512]{2,1,0:T(8,128)(2,1)} %param.19) | copy-start | bytes 6291460
  15.0 55.7 %copy-start.5 = (s32[512,1]{0,1:T(1,128)}, s32[512,1]{0,1:T(1,128)S(1)}, u32[]{:S(2)}) copy-start(s32[512,1]{0,1:T(1,128)S(1)} %compare_select_fusion) | copy-start | bytes 6148
  18.5 41.8 %all-to-all-start = ((bf16[64,16,512]{2,1,0:T(8,128)(2,1)}), bf16[64,16,512]{2,1,0:T(8,128)(2,1)}, u32[]{:S(2)}, u32[]{:S(2)}) async-start(bf16[64,16,512]{2,1,0:T(8,128)(2,1)} %bitcast.3), calls=%async_computation | async-start | bytes 2097152 | tf_op jit(solution)/shard_map/all_to_all | solution.py:99
  60.3 34.7 %all-to-all-start.2 = ((bf16[64,16,512]{2,1,0:T(8,128)(2,1)}), bf16[64,16,512]{2,1,0:T(8,128)(2,1)S(1)}, u32[]{:S(2)}, u32[]{:S(2)}) async-start(bf16[64,16,512]{2,1,0:T(8,128)(2,1)} %bitcast.9), calls=%async_computation.2 | async-start | bytes 2097152 | tf_op jit(solution)/shard_map/all_to_all | solution.py:105
  70.8 3.2 %copy-start.6 = (f32[1024,2048]{1,0:T(8,128)}, f32[1024,2048]{1,0:T(8,128)S(1)}, u32[]{:S(2)}) copy-start(f32[1024,2048]{1,0:T(8,128)S(1)} %fusion.14) | copy-start | bytes 25165828
  95.0 1.0 copy-start.1
  96.0 34.7 %all-to-all-start.1 = ((bf16[64,16,512]{2,1,0:T(8,128)(2,1)}), bf16[64,16,512]{2,1,0:T(8,128)(2,1)S(1)}, u32[]{:S(2)}, u32[]{:S(2)}) async-start(bf16[64,16,512]{2,1,0:T(8,128)(2,1)} %bitcast.65), calls=%async_computation.1 | async-start | bytes 2097152 | tf_op jit(solution)/shard_map/all_to_all | solution.py:102
  102.2 119.2 %all-reduce.3.cloned.1.call-start = ((), (), s32[]{:S(2)}) async-start(), calls=%async_computation.4 | async-start | bytes 8388608 | tf_op jit(solution)/shard_map/psum | solution.py:50
  111.0 2.0 copy-start.8
  113.0 5.2 %copy-start.2 = (bf16[64,16,512]{2,1,0:T(8,128)(2,1)S(1)}, bf16[64,16,512]{2,1,0:T(8,128)(2,1)}, u32[]{:S(2)}) copy-start(bf16[64,16,512]{2,1,0:T(8,128)(2,1)} %copy-done.1) | copy-start | bytes 3145732
  113.0 5.2 %copy-start.7 = (f32[1024,2048]{1,0:T(8,128)S(1)}, f32[1024,2048]{1,0:T(8,128)}, u32[]{:S(2)}) copy-start(f32[1024,2048]{1,0:T(8,128)} %copy-done.6) | copy-start | bytes 25165828
  130.7 37.0 %all-to-all-start.3 = ((bf16[64,16,512]{2,1,0:T(8,128)(2,1)}), bf16[64,16,512]{2,1,0:T(8,128)(2,1)}, u32[]{:S(2)}, u32[]{:S(2)}) async-start(bf16[64,16,512]{2,1,0:T(8,128)(2,1)} %bitcast.66), calls=%async_computation.3 | async-start | bytes 2097152 | tf_op jit(solution)/shard_map/all_to_all | solution.py:110
  141.1 35.2 %copy-start.4 = (s32[256,2]{0,1:T(2,128)S(1)}, s32[256,2]{0,1:T(2,128)}, u32[]{:S(2)}) copy-start(s32[256,2]{0,1:T(2,128)} %param.12) | copy-start | bytes 6148
  150.1 28.1 %copy-start.3 = (bf16[512,64]{0,1:T(8,128)(2,1)S(1)}, bf16[512,64]{0,1:T(8,128)(2,1)}, u32[]{:S(2)}) copy-start(bf16[512,64]{0,1:T(8,128)(2,1)} %param.17) | copy-start | bytes 196612
Sparse Core Ops, SparseCore 0:
  122.6 98.6 all-reduce.2
where the time goes:
time: 236 us; the launch traced here: 234 us
  waiting for transfers between devices  95.2 us (40%)
  matrix products  39.4 us (17%)
  starting transfers between devices  34.3 us (15%)
  local copies, waits for them, and re-layouts  32.2 us (14%)
  other arithmetic  19 us (8%)
  between operations  14.2 us (6%)
    psum x1, waiting for transfers between devices, expert_backward(): lax.psum(grad_up_part.astype(jnp.bfloat16), 'dp').astype(jnp.float32)  41 us
    all_to_all x1, waiting for transfers between devices, per_device(): lax.all_to_all(send_in, 'expert', split_axis=0, concat_axis=0, tiled=True)  18.6 us
    all_to_all x1, waiting for transfers between devices, per_device(): lax.all_to_all(send_cot, 'expert', split_axis=0, concat_axis=0, tiled=True)  17.1 us
    all_to_all x1, waiting for transfers between devices, per_device(): lax.all_to_all(d_inputs.reshape(buffer_shape), 'expert', split_axis=0, co...  16.6 us
    dot_general x2, matrix products, contract_cols(): lax.dot_general(left, right, (((1,), (1,)), ((), ())), preferred_element_...  15 us
    all_to_all x1, starting transfers between devices, per_device(): lax.all_to_all(send_in, 'expert', split_axis=0, concat_axis=0, tiled=True)  13.3 us
    unnamed x21, local copies, waits for them, and re-layouts  13.2 us
    dot_general x2, matrix products, contract_rows(): lax.dot_general(left, right, (((0,), (0,)), ((), ())), preferred_element_...  9.5 us
  transfers between devices with their start and end apart: 5, of which 5 were waited for; matrix products, arithmetic and copies ran while one was open for 29% of the time, Pallas kernels for 0%

commit v1 on v0

--- a/solution.py
+++ b/solution.py
@@ -81,41 +81,33 @@
     before = jnp.cumsum(flat_hot, axis=0, dtype=jnp.int32) - flat_hot
     slot_rank = jnp.sum(before * flat_hot, axis=1, dtype=jnp.int32)
     slot_place = flat_routes * capacity + slot_rank
-    buffer_shape = (n_experts, capacity, feature_width)
-    send_in = (
-        jnp.zeros((n_experts * capacity, feature_width), jnp.bfloat16)
-        .at[slot_place]
-        .set(jnp.repeat(mixed_in, TOP, axis=0))
-        .reshape(buffer_shape)
-    )
-    send_cot = (
-        jnp.zeros((n_experts * capacity, feature_width), jnp.bfloat16)
-        .at[slot_place]
-        .set(slot_cot.reshape(-1, feature_width))
-        .reshape(buffer_shape)
+    pair_shape = (n_experts, 2 * capacity, feature_width)
+    cot_place = slot_place + flat_routes * capacity + capacity
+    in_place = slot_place + flat_routes * capacity
+    send_rows = jnp.concatenate([jnp.repeat(mixed_in, TOP, axis=0), slot_cot.reshape(-1, feature_width)])
+    send_pair = (
+        jnp.zeros((n_experts * 2 * capacity, feature_width), jnp.bfloat16)
+        .at[jnp.concatenate([in_place, cot_place])]
+        .set(send_rows)
+        .reshape(pair_shape)
     )
     w_up_one = w_up[0]
     w_down_one = w_down[0]
-    recv_in = lax.all_to_all(send_in, "expert", split_axis=0, concat_axis=0, tiled=True)
-    flat_in = recv_in.reshape(-1, feature_width)
+    recv_pair = lax.all_to_all(send_pair, "expert", split_axis=0, concat_axis=0, tiled=True)
+    flat_in = recv_pair[:, :capacity].reshape(-1, feature_width)
+    flat_cot = recv_pair[:, capacity:].reshape(-1, feature_width)
     hidden, gelu_slope, outputs = expert_forward(flat_in, w_up_one, w_down_one)
-    back_out = lax.all_to_all(
-        outputs.reshape(buffer_shape), "expert", split_axis=0, concat_axis=0, tiled=True
-    )
-    recv_cot = lax.all_to_all(send_cot, "expert", split_axis=0, concat_axis=0, tiled=True)
-    flat_cot = recv_cot.reshape(-1, feature_width)
     d_inputs, sum_up, sum_down = expert_backward(
         flat_in, flat_cot, hidden, gelu_slope, w_up_one, w_down_one
     )
-    back_grad = lax.all_to_all(
-        d_inputs.reshape(buffer_shape), "expert", split_axis=0, concat_axis=0, tiled=True
+    back_pair = jnp.concatenate(
+        [outputs.reshape(n_experts, capacity, feature_width), d_inputs.reshape(n_experts, capacity, feature_width)],
+        axis=1,
     )
-    expert_out = back_out.reshape(-1, feature_width)[slot_place].reshape(
-        tok_rows, TOP, feature_width
-    )
-    slot_grad = back_grad.reshape(-1, feature_width)[slot_place].reshape(
-        tok_rows, TOP, feature_width
-    )
+    back_pair = lax.all_to_all(back_pair, "expert", split_axis=0, concat_axis=0, tiled=True)
+    back_flat = back_pair.reshape(-1, feature_width)
+    expert_out = back_flat[in_place].reshape(tok_rows, TOP, feature_width)
+    slot_grad = back_flat[cot_place].reshape(tok_rows, TOP, feature_width)
     expert_wide = expert_out.astype(jnp.float32)
     layer_out = (
         mixed_in.astype(jnp.float32) + jnp.sum(gates[:, :, None] * expert_wide, axis=1)

time: 236 us -> 245 us (1.038)
  blocking collectives: 0 us -> 64.5 us
  starting transfers between devices: 34.3 us -> 6.28 us
  waiting for transfers between devices: 95.2 us -> 72.7 us
  local copies, waits for them, and re-layouts: 32.2 us -> 26.7 us
  other arithmetic: 19 us -> 23.2 us
  matrix products: 39.4 us -> 36.2 us
    all_to_all x0 -> x1, blocking collectives: none -> 64.5 us  [per_device(): lax.all_to_all(send_pair, 'expert', split_axis=0, concat_axis=0, tiled=True)]
    all_to_all x4 -> x1, starting transfers between devices: 34.3 us -> 6.02 us  [per_device(): lax.all_to_all(back_pair, 'expert', split_axis=0, concat_axis=0, tiled=True)]
    all_to_all x4 -> x1, waiting for transfers between devices: 54.2 us -> 34.1 us  [per_device(): lax.all_to_all(back_pair, 'expert', split_axis=0, concat_axis=0, tiled=True)]
    dot_general x2, matrix products: 15 us -> 9.25 us  [contract_cols(): lax.dot_general(left, right, (((1,), (1,)), ((), ())), preferred_element_...]
    unnamed x21 -> x23, local copies, waits for them, and re-layouts: 13.2 us -> 7.52 us
    dot_general x2, matrix products: 9.5 us -> 14.6 us  [contract_rows(): lax.dot_general(left, right, (((0,), (0,)), ((), ())), preferred_element_...]
    scatter x1 -> x0, local copies, waits for them, and re-layouts: 3.47 us -> none  [per_device(): send_in = jnp.zeros((n_experts * capacity, feature_width), jnp.bfloat16)....]
    scatter x1, other arithmetic: 4.3 us -> 7.54 us  [per_device(): send_pair = jnp.zeros((n_experts * 2 * capacity, feature_width), jnp.bflo...]
  transfers between devices with their start and end apart: 5 -> 2, of which waited for: 5 -> 2; matrix products, arithmetic and copies ran while one was open for 29% -> 16% of each run, Pallas kernels for 0% -> 0%
where the time goes in v1:
time: 245 us; the launch traced here: 244 us
  waiting for transfers between devices  72.7 us (30%)
  blocking collectives  64.5 us (26%)
  matrix products  36.2 us (15%)
  local copies, waits for them, and re-layouts  26.7 us (11%)
  other arithmetic  23.2 us (9%)
  between operations  14.3 us (6%)
  starting transfers between devices  6.28 us (3%)
    all_to_all x1, blocking collectives, per_device(): lax.all_to_all(send_pair, 'expert', split_axis=0, concat_axis=0, tiled=True)  64.5 us
    psum x1, waiting for transfers between devices, expert_backward(): lax.psum(grad_up_part.astype(jnp.bfloat16), 'dp').astype(jnp.float32)  38.7 us
    all_to_all x1, waiting for transfers between devices, per_device(): lax.all_to_all(back_pair, 'expert', split_axis=0, concat_axis=0, tiled=True)  34.1 us
    dot_general x2, matrix products, contract_rows(): lax.dot_general(left, right, (((0,), (0,)), ((), ())), preferred_element_...  14.6 us
    dot_general x2, matrix products, contract_cols(): lax.dot_general(left, right, (((1,), (1,)), ((), ())), preferred_element_...  9.25 us
    scatter x1, other arithmetic, per_device(): send_pair = jnp.zeros((n_experts * 2 * capacity, feature_width), jnp.bflo...  7.54 us
    unnamed x23, local copies, waits for them, and re-layouts  7.52 us
    all_to_all x1, starting transfers between devices, per_device(): lax.all_to_all(back_pair, 'expert', split_axis=0, concat_axis=0, tiled=True)  6.02 us
  transfers between devices with their start and end apart: 2, of which 2 were waited for; matrix products, arithmetic and copies ran while one was open for 16% of the time, Pallas kernels for 0%

profile of v1, /device:TPU:1, one launch (start us, length us, event | category | flops | bytes accessed | tf_op | source)
XLA Modules:
  0.0 243.8 jit_solution(15967860060472708431)
XLA Ops:
  8.5 1.2 reduce-window.6
  11.6 1.2 fusion.37
  12.7 1.4 fusion.22
  14.1 1.0 fusion.38
  17.1 1.0 reshape.275
  18.0 1.2 mul.152
  19.3 1.7 mul.153
  21.7 1.4 multiply_convert_fusion.1
  23.0 7.5 %scatter_custom_fusion = bf16[2048,512]{1,0:T(8,128)(2,1)} fusion(s32[1024]{0:T(1024)S(1)} %bitcast.77, bf16[512,512]{1,0:T(8,128)(2,1)S(1)} %multiply_convert_fusion.1, bf16[]{:T(256)} %constant.35, bf16[512,512]{1,0:T(8,128)(2,1)} %reshape.275, bf16[]{:T(256)} %constant.13.clone.1), kind=kCustom, calls=%fused_computation.32 | custom fusion | flops 2097152 | bytes 3145732 | tf_op jit(solution)/shard_map/scatter | solution.py:91
  30.6 64.5 %all_to_all.10 = bf16[64,32,512]{2,1,0:T(8,128)(2,1)S(1)} all-to-all(bf16[64,32,512]{2,1,0:T(8,128)(2,1)} %bitcast.65), channel_id=1, replica_groups=mesh['dp'=4,'expert'=64] {'expert'}, dimensions={0} | all-to-all | bytes 4194304 | tf_op jit(solution)/shard_map/all_to_all | solution.py:96
  95.2 1.0 copy-done.3
  96.2 2.3 fusion.14
  98.6 3.2 %fusion.19 = bf16[1024,512]{1,0:T(8,128)(2,1)S(1)} fusion(bf16[1,2048,512]{2,1,0:T(8,128)(2,1)S(1)} %copy-done, f32[1024,2048]{1,0:T(8,128)S(1)} %fusion.14), kind=kOutput, calls=%fused_computation.26 | convolution fusion | flops 2166882304 | bytes 11534336 | tf_op jit(solution)/shard_map/dot_general | solution.py:39
  101.8 6.9 %fusion.6 = bf16[1024,2048]{1,0:T(8,128)(2,1)S(1)} fusion(f32[1024,2048]{1,0:T(8,128)S(1)} %fusion.14, bf16[1024,512]{1,0:T(8,128)(2,1)S(1)} %bitcast.66, bf16[1,2048,512]{2,1,0:T(8,128)(2,1)S(1)} %copy-done), kind=kOutput, calls=%fused_computation.11 | convolution fusion | flops 2187329536 | bytes 15728640 | tf_op jit(solution)/shard_map/dot_general | solution.py:30
  108.7 2.4 fusion.16
  111.1 1.5 pad_maximum_fusion
  112.6 6.0 %all-to-all-start.1 = ((bf16[64,32,512]{2,1,0:T(8,128)(2,1)}), bf16[64,32,512]{2,1,0:T(8,128)(2,1)}, u32[]{:S(2)}, u32[]{:S(2)}) async-start(bf16[64,32,512]{2,1,0:T(8,128)(2,1)} %pad_maximum_fusion), calls=%async_computation.1 | async-start | bytes 4194304 | tf_op jit(solution)/shard_map/all_to_all | solution.py:107
  118.9 6.2 %fusion.7 = bf16[1,512,2048]{2,1,0:T(8,128)(2,1)} fusion(bf16[1024,512]{1,0:T(8,128)(2,1)} %bitcast.69, bf16[1024,2048]{1,0:T(8,128)(2,1)} %copy-done.9), kind=kOutput, calls=%fused_computation.15 | convolution fusion | flops 2148532224 | bytes 7340032 | tf_op jit(solution)/shard_map/dot_general | solution.py:24
  125.1 8.4 %fusion.8 = bf16[1,2048,512]{2,1,0:T(8,128)(2,1)} fusion(bf16[1024,512]{1,0:T(8,128)(2,1)S(1)} %bitcast.67, f32[1024,2048]{1,0:T(8,128)} %copy-done.8), kind=kOutput, calls=%fused_computation.16 | convolution fusion | flops 2167406592 | bytes 11534336 | tf_op jit(solution)/shard_map/dot_general | solution.py:24
  135.7 34.1 %all-to-all-done.1 = bf16[64,32,512]{2,1,0:T(8,128)(2,1)} async-done(((bf16[64,32,512]{2,1,0:T(8,128)(2,1)}), bf16[64,32,512]{2,1,0:T(8,128)(2,1)}, u32[]{:S(2)}, u32[]{:S(2)}) %all-to-all-start.1) | async-done | bytes 2097184 | tf_op jit(solution)/shard_map/all_to_all | solution.py:107
  169.7 4.8 %gather_fusion.1 = bf16[512,512]{1,0:T(8,128)(2,1)} fusion(bf16[2048,512]{1,0:T(8,128)(2,1)} %bitcast.11, s32[1024]{0:T(1024)S(1)} %pad_clamp_fusion), kind=kCustom, calls=%fused_computation.1 | custom fusion | bytes 1050624 | tf_op jit(solution)/shard_map/gather | solution.py:110
  174.5 4.5 %gather_fusion = bf16[512,512]{1,0:T(8,128)(2,1)} fusion(bf16[2048,512]{1,0:T(8,128)(2,1)} %bitcast.11, s32[1024]{0:T(1024)S(1)} %pad_clamp_fusion.1), kind=kCustom, calls=%fused_computation | custom fusion | bytes 1050624 | tf_op jit(solution)/shard_map/gather | solution.py:109
  179.0 1.7 reshape.285
  180.7 3.9 %multiply_reduce_fusion = (f32[256,2]{1,0:T(8,128)}, f32[256,512]{1,0:T(8,128)}) fusion(f32[256,2,512]{2,1,0:T(2,128)S(1)} %reshape.285, f32[256,512]{1,0:T(8,128)} %convert_element_type.75, f32[256,2]{1,0:T(8,128)S(1)} %copy.28), kind=kLoop, calls=%fused_computation.36 | loop fusion | flops 916992 | bytes 2101248 | tf_op jit(solution)/shard_map/reduce_sum | solution.py:115
  184.7 1.0 copy.35
  185.7 1.7 reshape.286
  187.4 2.1 reduce_sum.79
  189.6 1.8 add_convert_fusion
  191.4 2.2 fusion.23
  193.7 38.7 %all-reduce.3.cloned.1.call-done = (bf16[1,512,2048]{2,1,0:T(8,128)(2,1)}, bf16[1,2048,512]{2,1,0:T(8,128)(2,1)}) async-done(((bf16[1,512,2048]{2,1,0:T(8,128)(2,1)}, bf16[1,2048,512]{2,1,0:T(8,128)(2,1)}), (bf16[1,512,2048]{2,1,0:T(8,128)(2,1)}, bf16[1,2048,512]{2,1,0:T(8,128)(2,1)})) %all-reduce.3.cloned.1.call-update) | async-done | bytes 4194320 | tf_op jit(solution)/shard_map/psum | solution.py:50
  232.4 3.3 %copy.40 = bf16[1,512,2048]{2,1,0:T(8,128)(2,1)} copy(bf16[1,512,2048]{2,1,0:T(8,128)(2,1)} %get-tuple-element.18) | data formatting | bytes 4194304
  235.7 1.3 copy.41
  (49 shorter events, 8.4 us)
Async XLA Ops:
  7.2 91.4 %copy-start = (bf16[1,2048,512]{2,1,0:T(8,128)(2,1)S(1)}, bf16[1,2048,512]{2,1,0:T(8,128)(2,1)}, u32[]{:S(2)}) copy-start(bf16[1,2048,512]{2,1,0:T(8,128)(2,1)} %param.19) | copy-start | bytes 6291460
  30.6 65.6 %copy-start.7 = (bf16[1,512,2048]{2,1,0:T(8,128)(2,1)S(1)}, bf16[1,512,2048]{2,1,0:T(8,128)(2,1)}, u32[]{:S(2)}) copy-start(bf16[1,512,2048]{2,1,0:T(8,128)(2,1)} %param.18) | copy-start | bytes 6291460
  95.2 1.0 copy-start.3
  98.6 3.2 %copy-start.8 = (f32[1024,2048]{1,0:T(8,128)}, f32[1024,2048]{1,0:T(8,128)S(1)}, u32[]{:S(2)}) copy-start(f32[1024,2048]{1,0:T(8,128)S(1)} %fusion.14) | copy-start | bytes 25165828
  108.7 2.4 copy-start.9
  112.6 57.1 %all-to-all-start.1 = ((bf16[64,32,512]{2,1,0:T(8,128)(2,1)}), bf16[64,32,512]{2,1,0:T(8,128)(2,1)}, u32[]{:S(2)}, u32[]{:S(2)}) async-start(bf16[64,32,512]{2,1,0:T(8,128)(2,1)} %pad_maximum_fusion), calls=%async_computation.1 | async-start | bytes 4194304 | tf_op jit(solution)/shard_map/all_to_all | solution.py:107
  118.6 113.7 %all-reduce.3.cloned.1.call-start = ((), (), s32[]{:S(2)}) async-start(), calls=%async_computation.2 | async-start | bytes 8388608 | tf_op jit(solution)/shard_map/psum | solution.py:50
  133.5 0.9 copy-start.1
  133.5 1.8 copy-start.5
  179.0 10.5 %copy-start.6 = (f32[256,2]{0,1:T(2,128)S(1)}, f32[256,2]{0,1:T(2,128)}, u32[]{:S(2)}) copy-start(f32[256,2]{0,1:T(2,128)} %get-tuple-element.9) | copy-start | bytes 6148
  184.7 6.8 %copy-start.4 = (bf16[512,64]{0,1:T(8,128)(2,1)S(1)}, bf16[512,64]{0,1:T(8,128)(2,1)}, u32[]{:S(2)}) copy-start(bf16[512,64]{0,1:T(8,128)(2,1)} %param.17) | copy-start | bytes 196612
  232.3 3.3 %copy-start.2 = (bf16[1,2048,512]{2,1,0:T(8,128)(2,1)S(1)}, bf16[1,2048,512]{2,1,0:T(8,128)(2,1)}, u32[]{:S(2)}) copy-start(bf16[1,2048,512]{2,1,0:T(8,128)(2,1)} %get-tuple-element.19) | copy-start | bytes 6291460
Sparse Core Ops, SparseCore 0:
  133.6 98.6 all-reduce.2

commit v2 on v1

--- a/solution.py
+++ b/solution.py
@@ -46,11 +46,7 @@
     d_pre = (d_hidden * gelu_slope).astype(jnp.bfloat16)
     d_inputs = contract_cols(d_pre, w_up_one).astype(jnp.bfloat16)
     grad_up_part = contract_rows(flat_in, d_pre)
-    sum_up, sum_down = (
-        lax.psum(grad_up_part.astype(jnp.bfloat16), "dp").astype(jnp.float32),
-        lax.psum(grad_down_part.astype(jnp.bfloat16), "dp").astype(jnp.float32),
-    )
-    return (d_inputs, sum_up, sum_down)
+    return (d_inputs, grad_up_part, grad_down_part)
 
 
 def per_device(
@@ -81,31 +77,41 @@
     before = jnp.cumsum(flat_hot, axis=0, dtype=jnp.int32) - flat_hot
     slot_rank = jnp.sum(before * flat_hot, axis=1, dtype=jnp.int32)
     slot_place = flat_routes * capacity + slot_rank
-    pair_shape = (n_experts, 2 * capacity, feature_width)
-    cot_place = slot_place + flat_routes * capacity + capacity
-    in_place = slot_place + flat_routes * capacity
+    half = capacity // 2
+    chunk_shape = (n_experts, 2 * half, feature_width)
+    in_place = flat_routes * (2 * capacity) + (slot_rank // half) * (2 * half) + slot_rank % half
+    cot_place = in_place + half
     send_rows = jnp.concatenate([jnp.repeat(mixed_in, TOP, axis=0), slot_cot.reshape(-1, feature_width)])
     send_pair = (
         jnp.zeros((n_experts * 2 * capacity, feature_width), jnp.bfloat16)
         .at[jnp.concatenate([in_place, cot_place])]
         .set(send_rows)
-        .reshape(pair_shape)
+        .reshape(n_experts, 2 * capacity, feature_width)
     )
     w_up_one = w_up[0]
     w_down_one = w_down[0]
-    recv_pair = lax.all_to_all(send_pair, "expert", split_axis=0, concat_axis=0, tiled=True)
-    flat_in = recv_pair[:, :capacity].reshape(-1, feature_width)
-    flat_cot = recv_pair[:, capacity:].reshape(-1, feature_width)
-    hidden, gelu_slope, outputs = expert_forward(flat_in, w_up_one, w_down_one)
-    d_inputs, sum_up, sum_down = expert_backward(
-        flat_in, flat_cot, hidden, gelu_slope, w_up_one, w_down_one
-    )
-    back_pair = jnp.concatenate(
-        [outputs.reshape(n_experts, capacity, feature_width), d_inputs.reshape(n_experts, capacity, feature_width)],
-        axis=1,
-    )
-    back_pair = lax.all_to_all(back_pair, "expert", split_axis=0, concat_axis=0, tiled=True)
-    back_flat = back_pair.reshape(-1, feature_width)
+    backs = []
+    grad_ups = []
+    grad_downs = []
+    for chunk in range(2):
+        sent = send_pair[:, chunk * 2 * half:(chunk + 1) * 2 * half]
+        recv = lax.all_to_all(sent, "expert", split_axis=0, concat_axis=0, tiled=True)
+        flat_in = recv[:, :half].reshape(-1, feature_width)
+        flat_cot = recv[:, half:].reshape(-1, feature_width)
+        hidden, gelu_slope, outputs = expert_forward(flat_in, w_up_one, w_down_one)
+        d_inputs, grad_up_part, grad_down_part = expert_backward(
+            flat_in, flat_cot, hidden, gelu_slope, w_up_one, w_down_one
+        )
+        grad_ups.append(grad_up_part)
+        grad_downs.append(grad_down_part)
+        back = jnp.concatenate(
+            [outputs.reshape(n_experts, half, feature_width), d_inputs.reshape(n_experts, half, feature_width)],
+            axis=1,
+        )
+        backs.append(lax.all_to_all(back, "expert", split_axis=0, concat_axis=0, tiled=True))
+    sum_up = lax.psum((grad_ups[0] + grad_ups[1]).astype(jnp.bfloat16), "dp")
+    sum_down = lax.psum((grad_downs[0] + grad_downs[1]).astype(jnp.bfloat16), "dp")
+    back_flat = jnp.concatenate(backs, axis=1).reshape(-1, feature_width)
     expert_out = back_flat[in_place].reshape(tok_rows, TOP, feature_width)
     slot_grad = back_flat[cot_place].reshape(tok_rows, TOP, feature_width)
     expert_wide = expert_out.astype(jnp.float32)

time: 245 us -> 246 us (level)
  blocking collectives: 64.5 us -> 41.6 us
  starting transfers between devices: 6.28 us -> 19.1 us
  local copies, waits for them, and re-layouts: 26.7 us -> 35.4 us
  other arithmetic: 23.2 us -> 30.2 us
  matrix products: 36.2 us -> 32.7 us
    all_to_all x1, blocking collectives: 64.5 us -> 41.6 us  [per_device(): lax.all_to_all(sent, 'expert', split_axis=0, concat_axis=0, tiled=True)]
    psum x1, waiting for transfers between devices: 38.7 us -> 24.3 us  [per_device(): sum_up = lax.psum((grad_ups[0] + grad_ups[1]).astype(jnp.bfloat16), 'dp')]
    all_to_all x1 -> x3, waiting for transfers between devices: 34.1 us -> 47.2 us  [the longest x2 28.4 us: per_device(): lax.all_to_all(back, 'expert', split_axis=0, concat_axis=0, tiled=True)]
    all_to_all x1 -> x3, starting transfers between devices: 6.02 us -> 18.8 us  [the longest x2 12.6 us: per_device(): lax.all_to_all(back, 'expert', split_axis=0, concat_axis=0, tiled=True)]
    dot_general x2 -> x4, matrix products: 14.6 us -> 8.89 us  [contract_rows(): lax.dot_general(left, right, (((0,), (0,)), ((), ())), preferred_element_...]
    concatenate x1 -> x3, other arithmetic: 1.48 us -> 5 us  [the longest x1 2.74 us: per_device(): back_flat = jnp.concatenate(backs, axis=1).reshape(-1, feature_width)]
    mul x2, local copies, waits for them, and re-layouts: 0.28 us -> 3.1 us  [per_device(): flat_routes * (2 * capacity) + slot_rank // half * (2 * half)]
    dot_general x1 -> x2, matrix products: 2.34 us -> 4.9 us  [expert_forward(): pre_act = jnp.dot(flat_in, w_up_one, preferred_element_type=jnp.float32)]
  transfers between devices with their start and end apart: 2 -> 4, of which waited for: 2 -> 4; matrix products, arithmetic and copies ran while one was open for 16% -> 26% of each run, Pallas kernels for 0% -> 0%
where the time goes in v2:
time: 246 us; the launch traced here: 245 us
  waiting for transfers between devices  71.5 us (29%)
  blocking collectives  41.6 us (17%)
  local copies, waits for them, and re-layouts  35.4 us (14%)
  matrix products  32.7 us (13%)
  other arithmetic  30.2 us (12%)
  starting transfers between devices  19.1 us (8%)
  between operations  14.5 us (6%)
    all_to_all x1, blocking collectives, per_device(): lax.all_to_all(sent, 'expert', split_axis=0, concat_axis=0, tiled=True)  41.6 us
    all_to_all x2, waiting for transfers between devices, per_device(): lax.all_to_all(back, 'expert', split_axis=0, concat_axis=0, tiled=True)  28.4 us
    psum x1, waiting for transfers between devices, per_device(): sum_up = lax.psum((grad_ups[0] + grad_ups[1]).astype(jnp.bfloat16), 'dp')  24.3 us
    all_to_all x1, waiting for transfers between devices, per_device(): lax.all_to_all(sent, 'expert', split_axis=0, concat_axis=0, tiled=True)  18.8 us
    all_to_all x2, starting transfers between devices, per_device(): lax.all_to_all(back, 'expert', split_axis=0, concat_axis=0, tiled=True)  12.6 us
    dot_general x4, matrix products, contract_cols(): lax.dot_general(left, right, (((1,), (1,)), ((), ())), preferred_element_...  10.8 us
    dot_general x4, matrix products, contract_rows(): lax.dot_general(left, right, (((0,), (0,)), ((), ())), preferred_element_...  8.89 us
    unnamed x51, local copies, waits for them, and re-layouts  7.7 us
  transfers between devices with their start and end apart: 4, of which 4 were waited for; matrix products, arithmetic and copies ran while one was open for 26% of the time, Pallas kernels for 0%

profile of v2, /device:TPU:1, one launch (start us, length us, event | category | flops | bytes accessed | tf_op | source)
XLA Modules:
  0.0 244.9 jit_solution(4124582627499485579)
XLA Ops:
  11.9 1.7 mul.241
  20.5 2.0 reshape.354
  25.4 7.4 %scatter_custom_fusion = bf16[2048,512]{1,0:T(8,128)(2,1)} fusion(s32[1024]{0:T(1024)} %bitcast.110, bf16[512,512]{1,0:T(8,128)(2,1)} %multiply_convert_fusion.2, bf16[]{:T(256)} %constant.67, bf16[512,512]{1,0:T(8,128)(2,1)} %reshape.354, bf16[]{:T(256)} %constant.49.clone.1), kind=kCustom, calls=%fused_computation.55 | custom fusion | flops 2097152 | bytes 3146752 | tf_op jit(solution)/shard_map/scatter | solution.py:88
  32.8 2.7 %fusion.78 = (bf16[64,16,512]{2,1,0:T(8,128)(2,1)}, bf16[64,16,512]{2,1,0:T(8,128)(2,1)S(1)}) fusion(bf16[64,32,512]{2,1,0:T(8,128)(2,1)} %bitcast.104), kind=kLoop, calls=%fused_computation.117 | loop fusion | bytes 4194304 | tf_op jit(solution)/shard_map/slice | solution.py:97
  35.5 41.6 %all_to_all.20 = bf16[64,16,512]{2,1,0:T(8,128)(2,1)} all-to-all(bf16[64,16,512]{2,1,0:T(8,128)(2,1)S(1)} %get-tuple-element.15), channel_id=1, replica_groups=mesh['dp'=4,'expert'=64] {'expert'}, dimensions={0} | all-to-all | bytes 2097152 | tf_op jit(solution)/shard_map/all_to_all | solution.py:98
  77.1 6.2 %all-to-all-start = ((bf16[64,16,512]{2,1,0:T(8,128)(2,1)}), bf16[64,16,512]{2,1,0:T(8,128)(2,1)S(1)}, u32[]{:S(2)}, u32[]{:S(2)}) async-start(bf16[64,16,512]{2,1,0:T(8,128)(2,1)} %get-tuple-element.14), calls=%async_computation | async-start | bytes 2097152 | tf_op jit(solution)/shard_map/all_to_all | solution.py:98
  83.3 2.4 fusion.24
  85.8 3.3 %fusion.13 = bf16[512,2048]{1,0:T(8,128)(2,1)S(1)} fusion(f32[512,2048]{1,0:T(8,128)S(1)} %fusion.24, bf16[1,2048,512]{2,1,0:T(8,128)(2,1)S(1)} %copy-done.19, bf16[64,16,512]{2,1,0:T(8,128)(2,1)S(1)} %copy-done.8), kind=kOutput, calls=%fused_computation.20 | convolution fusion | flops 1093664768 | bytes 8912896 | tf_op jit(solution)/shard_map/dot_general | solution.py:30
  93.0 18.8 %all-to-all-done = bf16[64,16,512]{2,1,0:T(8,128)(2,1)S(1)} async-done(((bf16[64,16,512]{2,1,0:T(8,128)(2,1)}), bf16[64,16,512]{2,1,0:T(8,128)(2,1)S(1)}, u32[]{:S(2)}, u32[]{:S(2)}) %all-to-all-start) | async-done | bytes 1048608 | tf_op jit(solution)/shard_map/all_to_all | solution.py:98
  112.8 6.2 %all-to-all-start.3 = ((bf16[64,16,512]{2,1,0:T(8,128)(2,1)}), bf16[64,16,512]{2,1,0:T(8,128)(2,1)S(1)}, u32[]{:S(2)}, u32[]{:S(2)}) async-start(bf16[64,16,512]{2,1,0:T(8,128)(2,1)} %pad_maximum_fusion.2), calls=%async_computation.3 | async-start | bytes 2097152 | tf_op jit(solution)/shard_map/all_to_all | solution.py:111
  119.3 2.4 fusion.28
  121.8 3.3 %fusion.6 = bf16[512,2048]{1,0:T(8,128)(2,1)S(1)} fusion(f32[512,2048]{1,0:T(8,128)S(1)} %fusion.28, bf16[1,2048,512]{2,1,0:T(8,128)(2,1)S(1)} %copy-done.20, bf16[64,16,512]{2,1,0:T(8,128)(2,1)S(1)} %copy-done.7), kind=kOutput, calls=%fused_computation.13 | convolution fusion | flops 1093664768 | bytes 8912896 | tf_op jit(solution)/shard_map/dot_general | solution.py:30
  125.1 1.8 fusion.62
  128.9 2.7 %fusion.14 = bf16[1,512,2048]{2,1,0:T(8,128)(2,1)} fusion(f32[512,2048]{1,0:T(8,128)S(1)} %fusion.61, bf16[512,2048]{1,0:T(8,128)(2,1)S(1)} %copy-done.23, bf16[64,16,512]{2,1,0:T(8,128)(2,1)S(1)} %copy-done.9), kind=kOutput, calls=%fused_computation.25 | convolution fusion | flops 1075838976 | bytes 8912896 | tf_op jit(solution)/shard_map/dot_general | solution.py:24
  131.6 3.1 %fusion.15 = bf16[1,2048,512]{2,1,0:T(8,128)(2,1)} fusion(f32[2048,512]{1,0:T(8,128)S(1)} %fusion.62, bf16[64,16,512]{2,1,0:T(8,128)(2,1)S(1)} %copy-done.9, f32[512,2048]{1,0:T(8,128)S(1)} %copy-done.3), kind=kOutput, calls=%fused_computation.26 | convolution fusion | flops 1085276160 | bytes 11010048 | tf_op jit(solution)/shard_map/dot_general | solution.py:24
  134.7 3.0 %fusion.51 = bf16[64,8,512]{2,1,0:T(8,128)(2,1)S(1)} fusion(bf16[512,2048]{1,0:T(8,128)(2,1)} %copy-done.11, bf16[1,512,2048]{2,1,0:T(8,128)(2,1)S(1)} %copy-done), kind=kOutput, calls=%fused_computation.49 | convolution fusion | flops 1074003968 | bytes 4718592 | tf_op jit(solution)/shard_map/dot_general | solution.py:30
  140.7 6.8 %all-to-all-done.3 = bf16[64,16,512]{2,1,0:T(8,128)(2,1)S(1)} async-done(((bf16[64,16,512]{2,1,0:T(8,128)(2,1)}), bf16[64,16,512]{2,1,0:T(8,128)(2,1)S(1)}, u32[]{:S(2)}, u32[]{:S(2)}) %all-to-all-start.3) | async-done | bytes 1048608 | tf_op jit(solution)/shard_map/all_to_all | solution.py:111
  147.5 6.4 %all-to-all-start.1 = ((bf16[64,16,512]{2,1,0:T(8,128)(2,1)}), bf16[64,16,512]{2,1,0:T(8,128)(2,1)}, u32[]{:S(2)}, u32[]{:S(2)}) async-start(bf16[64,16,512]{2,1,0:T(8,128)(2,1)} %pad_maximum_fusion.1), calls=%async_computation.1 | async-start | bytes 2097152 | tf_op jit(solution)/shard_map/all_to_all | solution.py:111
  153.9 1.8 convert_element_type.83
  157.8 1.6 mul.273
  160.7 21.6 %all-to-all-done.1 = bf16[64,16,512]{2,1,0:T(8,128)(2,1)} async-done(((bf16[64,16,512]{2,1,0:T(8,128)(2,1)}), bf16[64,16,512]{2,1,0:T(8,128)(2,1)}, u32[]{:S(2)}, u32[]{:S(2)}) %all-to-all-start.1) | async-done | bytes 1048608 | tf_op jit(solution)/shard_map/all_to_all | solution.py:111
  182.4 2.7 %pad_maximum_fusion = bf16[64,32,512]{2,1,0:T(8,128)(2,1)} fusion(bf16[64,16,512]{2,1,0:T(8,128)(2,1)S(1)} %all-to-all-done.3, bf16[64,16,512]{2,1,0:T(8,128)(2,1)} %all-to-all-done.1), kind=kLoop, calls=%fused_computation.27 | loop fusion | flops 4194304 | bytes 4194304 | tf_op jit(solution)/shard_map/concatenate | solution.py:114
  185.1 4.7 %gather_fusion = bf16[512,512]{1,0:T(8,128)(2,1)} fusion(bf16[2048,512]{1,0:T(8,128)(2,1)} %bitcast.102, s32[1024]{0:T(1024)} %pad_clamp_fusion.1), kind=kCustom, calls=%fused_computation | custom fusion | bytes 1050624 | tf_op jit(solution)/shard_map/gather | solution.py:115
  189.7 1.7 reshape.368
  191.4 3.9 %multiply_reduce_fusion = (f32[256,2]{1,0:T(8,128)}, f32[256,512]{1,0:T(8,128)}) fusion(f32[256,2,512]{2,1,0:T(2,128)S(1)} %reshape.368, f32[256,512]{1,0:T(8,128)} %convert_element_type.83, f32[256,2]{1,0:T(8,128)S(1)} %copy.28), kind=kLoop, calls=%fused_computation.61 | loop fusion | flops 916992 | bytes 2101248 | tf_op jit(solution)/shard_map/reduce_sum | solution.py:121
  196.4 4.8 %gather_fusion.1 = bf16[512,512]{1,0:T(8,128)(2,1)} fusion(bf16[2048,512]{1,0:T(8,128)(2,1)} %bitcast.103, s32[1024]{0:T(1024)S(1)} %pad_clamp_fusion), kind=kCustom, calls=%fused_computation.1 | custom fusion | bytes 1050624 | tf_op jit(solution)/shard_map/gather | solution.py:116
  201.2 1.7 reshape.369
  202.9 2.1 reduce_sum.79
  205.1 1.8 add_convert_fusion.2
  206.9 2.2 fusion.55
  209.1 24.3 %all-reduce.3.cloned.1.call-done = (bf16[1,512,2048]{2,1,0:T(8,128)(2,1)}, bf16[1,2048,512]{2,1,0:T(8,128)(2,1)}) async-done(((bf16[1,512,2048]{2,1,0:T(8,128)(2,1)}, bf16[1,2048,512]{2,1,0:T(8,128)(2,1)}), (bf16[1,512,2048]{2,1,0:T(8,128)(2,1)}, bf16[1,2048,512]{2,1,0:T(8,128)(2,1)})) %all-reduce.3.cloned.1.call-update) | async-done | bytes 4194320 | tf_op jit(solution)/shard_map/psum | solution.py:112
  233.4 3.3 %copy.40 = bf16[1,512,2048]{2,1,0:T(8,128)(2,1)} copy(bf16[1,512,2048]{2,1,0:T(8,128)(2,1)} %get-tuple-element.18) | data formatting | bytes 4194304
  (90 shorter events, 30.2 us)
Async XLA Ops:
  7.2 76.1 %copy-start = (bf16[1,512,2048]{2,1,0:T(8,128)(2,1)S(1)}, bf16[1,512,2048]{2,1,0:T(8,128)(2,1)}, u32[]{:S(2)}) copy-start(bf16[1,512,2048]{2,1,0:T(8,128)(2,1)} %param.18) | copy-start | bytes 6291460
  7.2 9.4 %copy-start.14 = (s32[256,2]{0,1:T(2,128)S(1)}, s32[256,2]{0,1:T(2,128)}, u32[]{:S(2)}) copy-start(s32[256,2]{0,1:T(2,128)} %param.12) | copy-start | bytes 6148
  7.2 6.4 %copy-start.16 = (bf16[32,64]{1,0:T(8,128)(2,1)S(1)}, bf16[32,64]{1,0:T(8,128)(2,1)}, u32[]{:S(2)}) copy-start(bf16[32,64]{1,0:T(8,128)(2,1)} %param.14) | copy-start | bytes 12292
  7.2 6.4 %copy-start.15 = (bf16[64,256]{1,0:T(8,128)(2,1)S(1)}, bf16[64,256]{1,0:T(8,128)(2,1)}, u32[]{:S(2)}) copy-start(bf16[64,256]{1,0:T(8,128)(2,1)} %param.15) | copy-start | bytes 98308
  7.2 7.8 %copy-start.18 = (s32[256]{0:T(256)S(1)}, s32[256]{0:T(256)}, u32[]{:S(2)}) copy-start(s32[256]{0:T(256)} %param.11) | copy-start | bytes 3076
  7.2 9.2 %copy-start.12 = (bf16[512,64]{0,1:T(8,128)(2,1)S(1)}, bf16[512,64]{0,1:T(8,128)(2,1)}, u32[]{:S(2)}) copy-start(bf16[512,64]{0,1:T(8,128)(2,1)} %param.17) | copy-start | bytes 196612
  13.6 10.2 %copy-start.1 = (f32[512,512]{1,0:T(8,128)S(1)}, f32[512,512]{1,0:T(8,128)}, u32[]{:S(2)}) copy-start(f32[512,512]{1,0:T(8,128)} %mul.241) | copy-start | bytes 3145732
  77.1 34.7 %all-to-all-start = ((bf16[64,16,512]{2,1,0:T(8,128)(2,1)}), bf16[64,16,512]{2,1,0:T(8,128)(2,1)S(1)}, u32[]{:S(2)}, u32[]{:S(2)}) async-start(bf16[64,16,512]{2,1,0:T(8,128)(2,1)} %get-tuple-element.14), calls=%async_computation | async-start | bytes 2097152 | tf_op jit(solution)/shard_map/all_to_all | solution.py:98
  83.3 2.5 %copy-start.8 = (bf16[64,16,512]{2,1,0:T(8,128)(2,1)S(1)}, bf16[64,16,512]{2,1,0:T(8,128)(2,1)}, u32[]{:S(2)}) copy-start(bf16[64,16,512]{2,1,0:T(8,128)(2,1)} %all_to_all.20) | copy-start | bytes 3145732
  83.3 2.5 %copy-start.19 = (bf16[1,2048,512]{2,1,0:T(8,128)(2,1)S(1)}, bf16[1,2048,512]{2,1,0:T(8,128)(2,1)}, u32[]{:S(2)}) copy-start(bf16[1,2048,512]{2,1,0:T(8,128)(2,1)} %param.19) | copy-start | bytes 6291460
  85.8 4.6 %copy-start.2 = (f32[512,2048]{1,0:T(8,128)}, f32[512,2048]{1,0:T(8,128)S(1)}, u32[]{:S(2)}) copy-start(f32[512,2048]{1,0:T(8,128)S(1)} %fusion.24) | copy-start | bytes 12582916
  89.1 1.3 copy-start.22
  111.8 1.0 copy-start.6
  112.8 34.7 %all-to-all-start.3 = ((bf16[64,16,512]{2,1,0:T(8,128)(2,1)}), bf16[64,16,512]{2,1,0:T(8,128)(2,1)S(1)}, u32[]{:S(2)}, u32[]{:S(2)}) async-start(bf16[64,16,512]{2,1,0:T(8,128)(2,1)} %pad_maximum_fusion.2), calls=%async_computation.3 | async-start | bytes 2097152 | tf_op jit(solution)/shard_map/all_to_all | solution.py:111
  119.0 114.4 %all-reduce.3.cloned.1.call-start = ((), (), s32[]{:S(2)}) async-start(), calls=%async_computation.4 | async-start | bytes 8388608 | tf_op jit(solution)/shard_map/psum | solution.py:112
  119.3 2.5 %copy-start.7 = (bf16[64,16,512]{2,1,0:T(8,128)(2,1)S(1)}, bf16[64,16,512]{2,1,0:T(8,128)(2,1)}, u32[]{:S(2)}) copy-start(bf16[64,16,512]{2,1,0:T(8,128)(2,1)} %copy-done.6) | copy-start | bytes 3145732
  119.3 2.5 %copy-start.20 = (bf16[1,2048,512]{2,1,0:T(8,128)(2,1)S(1)}, bf16[1,2048,512]{2,1,0:T(8,128)(2,1)}, u32[]{:S(2)}) copy-start(bf16[1,2048,512]{2,1,0:T(8,128)(2,1)} %param.19) | copy-start | bytes 6291460
  121.8 3.3 %copy-start.4 = (f32[512,2048]{1,0:T(8,128)}, f32[512,2048]{1,0:T(8,128)S(1)}, u32[]{:S(2)}) copy-start(f32[512,2048]{1,0:T(8,128)S(1)} %fusion.28) | copy-start | bytes 12582916
  125.1 1.9 copy-start.11
  126.9 1.3 copy-start.9
  126.9 1.9 copy-start.23
  128.9 2.7 %copy-start.3 = (f32[512,2048]{1,0:T(8,128)S(1)}, f32[512,2048]{1,0:T(8,128)}, u32[]{:S(2)}) copy-start(f32[512,2048]{1,0:T(8,128)} %copy-done.2) | copy-start | bytes 12582916
  134.6 3.1 %copy-start.5 = (f32[512,2048]{1,0:T(8,128)S(1)}, f32[512,2048]{1,0:T(8,128)}, u32[]{:S(2)}) copy-start(f32[512,2048]{1,0:T(8,128)} %copy-done.4) | copy-start | bytes 12582916
  134.6 3.5 %copy-start.21 = (bf16[1,2048,512]{2,1,0:T(8,128)(2,1)S(1)}, bf16[1,2048,512]{2,1,0:T(8,128)(2,1)}, u32[]{:S(2)}) copy-start(bf16[1,2048,512]{2,1,0:T(8,128)(2,1)} %param.19) | copy-start | bytes 6291460
  147.5 34.8 %all-to-all-start.1 = ((bf16[64,16,512]{2,1,0:T(8,128)(2,1)}), bf16[64,16,512]{2,1,0:T(8,128)(2,1)}, u32[]{:S(2)}, u32[]{:S(2)}) async-start(bf16[64,16,512]{2,1,0:T(8,128)(2,1)} %pad_maximum_fusion.1), calls=%async_computation.1 | async-start | bytes 2097152 | tf_op jit(solution)/shard_map/all_to_all | solution.py:111
  195.4 9.7 %copy-start.17 = (f32[256,2]{0,1:T(2,128)S(1)}, f32[256,2]{0,1:T(2,128)}, u32[]{:S(2)}) copy-start(f32[256,2]{0,1:T(2,128)} %get-tuple-element.11) | copy-start | bytes 6148
  196.4 10.5 %copy-start.13 = (bf16[512,64]{0,1:T(8,128)(2,1)S(1)}, bf16[512,64]{0,1:T(8,128)(2,1)}, u32[]{:S(2)}) copy-start(bf16[512,64]{0,1:T(8,128)(2,1)} %param.17) | copy-start | bytes 196612
  233.4 3.3 %copy-start.10 = (bf16[1,2048,512]{2,1,0:T(8,128)(2,1)S(1)}, bf16[1,2048,512]{2,1,0:T(8,128)(2,1)}, u32[]{:S(2)}) copy-start(bf16[1,2048,512]{2,1,0:T(8,128)(2,1)} %get-tuple-element.19) | copy-start | bytes 6291460
Sparse Core Ops, SparseCore 0:
  134.8 98.6 all-reduce.2

commit v3 on v2

--- a/solution.py
+++ b/solution.py
@@ -71,31 +71,36 @@
     gate_total = jnp.sum(squashed, axis=1, keepdims=True)
     gates = squashed / gate_total
     cot_wide = cotangent.astype(jnp.float32)
-    slot_cot = (gates[:, :, None] * cot_wide[:, None, :]).astype(jnp.bfloat16)
+    slot_cot = jnp.concatenate(
+        [(gates[:, k:k + 1] * cot_wide).astype(jnp.bfloat16) for k in range(TOP)]
+    )
     flat_routes = routes.reshape(-1)
     flat_hot = route_hot.reshape(-1, n_experts).astype(jnp.int32)
     before = jnp.cumsum(flat_hot, axis=0, dtype=jnp.int32) - flat_hot
-    slot_rank = jnp.sum(before * flat_hot, axis=1, dtype=jnp.int32)
-    slot_place = flat_routes * capacity + slot_rank
+    slot_rank = jnp.sum(before * flat_hot, axis=1, dtype=jnp.int32).reshape(tok_rows, TOP)
     half = capacity // 2
-    chunk_shape = (n_experts, 2 * half, feature_width)
-    in_place = flat_routes * (2 * capacity) + (slot_rank // half) * (2 * half) + slot_rank % half
-    cot_place = in_place + half
-    send_rows = jnp.concatenate([jnp.repeat(mixed_in, TOP, axis=0), slot_cot.reshape(-1, feature_width)])
-    send_pair = (
-        jnp.zeros((n_experts * 2 * capacity, feature_width), jnp.bfloat16)
-        .at[jnp.concatenate([in_place, cot_place])]
-        .set(send_rows)
-        .reshape(n_experts, 2 * capacity, feature_width)
-    )
+    rows_in = jnp.concatenate([mixed_in, slot_cot])
     w_up_one = w_up[0]
     w_down_one = w_down[0]
-    backs = []
+    spots = jnp.arange(n_experts * 2 * half, dtype=jnp.int32)
+    gathered = []
     grad_ups = []
     grad_downs = []
     for chunk in range(2):
-        sent = send_pair[:, chunk * 2 * half:(chunk + 1) * 2 * half]
-        recv = lax.all_to_all(sent, "expert", split_axis=0, concat_axis=0, tiled=True)
+        mine = slot_rank // half == chunk
+        in_spot = jnp.where(mine, routes * (2 * half) + slot_rank % half, -1)
+        cot_spot = jnp.where(mine, in_spot + half, -1)
+        pick = jnp.concatenate(
+            [
+                (spots[:, None] == in_spot[None, :, 0]) | (spots[:, None] == in_spot[None, :, 1]),
+                spots[:, None] == cot_spot.T.reshape(1, -1),
+            ],
+            axis=1,
+        ).astype(jnp.bfloat16)
+        sent = jnp.dot(pick, rows_in, preferred_element_type=jnp.float32).astype(jnp.bfloat16)
+        recv = lax.all_to_all(
+            sent.reshape(n_experts, 2 * half, feature_width), "expert", split_axis=0, concat_axis=0, tiled=True
+        )
         flat_in = recv[:, :half].reshape(-1, feature_width)
         flat_cot = recv[:, half:].reshape(-1, feature_width)
         hidden, gelu_slope, outputs = expert_forward(flat_in, w_up_one, w_down_one)
@@ -108,13 +113,21 @@
             [outputs.reshape(n_experts, half, feature_width), d_inputs.reshape(n_experts, half, feature_width)],
             axis=1,
         )
-        backs.append(lax.all_to_all(back, "expert", split_axis=0, concat_axis=0, tiled=True))
+        back = lax.all_to_all(back, "expert", split_axis=0, concat_axis=0, tiled=True)
+        take = jnp.concatenate(
+            [
+                in_spot.T.reshape(-1, 1) == spots[None, :],
+                (cot_spot[:, 0:1] == spots[None, :]) | (cot_spot[:, 1:2] == spots[None, :]),
+            ]
+        ).astype(jnp.bfloat16)
+        gathered.append(
+            jnp.dot(take, back.reshape(-1, feature_width), preferred_element_type=jnp.float32)
+        )
     sum_up = lax.psum((grad_ups[0] + grad_ups[1]).astype(jnp.bfloat16), "dp")
     sum_down = lax.psum((grad_downs[0] + grad_downs[1]).astype(jnp.bfloat16), "dp")
-    back_flat = jnp.concatenate(backs, axis=1).reshape(-1, feature_width)
-    expert_out = back_flat[in_place].reshape(tok_rows, TOP, feature_width)
-    slot_grad = back_flat[cot_place].reshape(tok_rows, TOP, feature_width)
-    expert_wide = expert_out.astype(jnp.float32)
+    picked = gathered[0] + gathered[1]
+    expert_wide = jnp.stack([picked[k * tok_rows:(k + 1) * tok_rows] for k in range(TOP)], axis=1)
+    grad_sum = picked[TOP * tok_rows:]
     layer_out = (
         mixed_in.astype(jnp.float32) + jnp.sum(gates[:, :, None] * expert_wide, axis=1)
     ).astype(jnp.bfloat16)
@@ -128,9 +141,7 @@
         (((1,), (1,)), ((), ())),
         precision=lax.Precision.HIGHEST,
     )
-    grad_in = (cot_wide + jnp.sum(slot_grad.astype(jnp.float32), axis=1) + d_router).astype(
-        jnp.bfloat16
-    )
+    grad_in = (cot_wide + grad_sum + d_router).astype(jnp.bfloat16)
     return (
         layer_out,
         grad_in,

time: 246 us -> 231 us (0.939)
  blocking collectives: 41.6 us -> 0 us
  waiting for transfers between devices: 71.5 us -> 112 us
  local copies, waits for them, and re-layouts: 35.4 us -> 6.5 us
  matrix products: 32.7 us -> 53.9 us
  other arithmetic: 30.2 us -> 10.6 us
  starting transfers between devices: 19.1 us -> 32.6 us
    all_to_all x1 -> x0, blocking collectives: 41.6 us -> none  [per_device(): lax.all_to_all(sent, 'expert', split_axis=0, concat_axis=0, tiled=True)]
    psum x1, waiting for transfers between devices: 24.3 us -> 46.8 us  [per_device(): sum_up = lax.psum((grad_ups[0] + grad_ups[1]).astype(jnp.bfloat16), 'dp')]
    all_to_all x1 -> x2, waiting for transfers between devices: 18.8 us -> 36.3 us  [per_device(): lax.all_to_all(sent.reshape(n_experts, 2 * half, feature_width), 'expert'...]
    all_to_all x1 -> x2, starting transfers between devices: 6.21 us -> 19.5 us  [per_device(): lax.all_to_all(sent.reshape(n_experts, 2 * half, feature_width), 'expert'...]
    dot_general x0 -> x4, matrix products: none -> 11.2 us  [the longest x2 6.25 us: per_device(): jnp.dot(take, back.reshape(-1, feature_width), preferred_element_type=jnp...]
    gather x2 -> x0, local copies, waits for them, and re-layouts: 9.44 us -> none  [the longest x1 4.79 us: per_device(): slot_grad = back_flat[cot_place].reshape(tok_rows, TOP, feature_width)]
    scatter x1 -> x0, other arithmetic: 7.43 us -> none  [per_device(): send_pair = jnp.zeros((n_experts * 2 * capacity, feature_width), jnp.bflo...]
    dot_general x4, matrix products: 8.89 us -> 15.3 us  [contract_rows(): lax.dot_general(left, right, (((0,), (0,)), ((), ())), preferred_element_...]
  transfers between devices with their start and end apart: 4 -> 5, of which waited for: 4 -> 5; matrix products, arithmetic and copies ran while one was open for 26% -> 23% of each run, Pallas kernels for 0% -> 0%
where the time goes in v3:
time: 231 us; the launch traced here: 230 us
  waiting for transfers between devices  112 us (48%)
  matrix products  53.9 us (23%)
  starting transfers between devices  32.6 us (14%)
  between operations  14.5 us (6%)
  other arithmetic  10.6 us (5%)
  local copies, waits for them, and re-layouts  6.5 us (3%)
    psum x1, waiting for transfers between devices, per_device(): sum_up = lax.psum((grad_ups[0] + grad_ups[1]).astype(jnp.bfloat16), 'dp')  46.8 us
    all_to_all x2, waiting for transfers between devices, per_device(): lax.all_to_all(sent.reshape(n_experts, 2 * half, feature_width), 'expert'...  36.3 us
    all_to_all x2, waiting for transfers between devices, per_device(): lax.all_to_all(back, 'expert', split_axis=0, concat_axis=0, tiled=True)  28.6 us
    all_to_all x2, starting transfers between devices, per_device(): lax.all_to_all(sent.reshape(n_experts, 2 * half, feature_width), 'expert'...  19.5 us
    dot_general x4, matrix products, contract_rows(): lax.dot_general(left, right, (((0,), (0,)), ((), ())), preferred_element_...  15.3 us
    all_to_all x2, starting transfers between devices, per_device(): lax.all_to_all(back, 'expert', split_axis=0, concat_axis=0, tiled=True)  12.8 us
    dot_general x4, matrix products, contract_cols(): lax.dot_general(left, right, (((1,), (1,)), ((), ())), preferred_element_...  10.7 us
    dot_general x2, matrix products, per_device(): jnp.dot(take, back.reshape(-1, feature_width), preferred_element_type=jnp...  6.25 us
  transfers between devices with their start and end apart: 5, of which 5 were waited for; matrix products, arithmetic and copies ran while one was open for 23% of the time, Pallas kernels for 0%

profile of v3, /device:TPU:1, one launch (start us, length us, event | category | flops | bytes accessed | tf_op | source)
XLA Modules:
  0.0 229.7 jit_solution(12192636545729154510)
XLA Ops:
  8.5 1.2 reduce-window.6
  11.9 1.2 fusion.107
  13.1 1.4 fusion.79
  18.1 2.0 fusion.52
  20.0 13.1 %all-to-all-start = ((bf16[64,16,512]{2,1,0:T(8,128)(2,1)}), bf16[64,16,512]{2,1,0:T(8,128)(2,1)S(1)}, u32[]{:S(2)}, u32[]{:S(2)}) async-start(bf16[64,16,512]{2,1,0:T(8,128)(2,1)} %bitcast.127), calls=%async_computation | async-start | bytes 2097152 | tf_op jit(solution)/shard_map/all_to_all | solution.py:101
  33.8 3.0 %fusion.46 = bf16[1024,512]{1,0:T(8,128)(2,1)} fusion(pred[1024,512]{1,0:T(32,128)(4,1)S(1)} %iota_compare_fusion, pred[1024,256]{1,0:T(32,128)(4,1)S(1)} %fusion.84, bf16[256,512]{1,0:T(8,128)(2,1)} %copy-done.8, bf16[256,512]{1,0:T(8,128)(2,1)} %copy-done.7, bf16[256,512]{1,0:T(8,128)(2,1)S(1)} %fusion.79), kind=kOutput, calls=%fused_computation.58 | convolution fusion | flops 808976384 | bytes 2621440 | tf_op jit(solution)/shard_map/dot_general | solution.py:100
  36.8 24.9 %all-to-all-done = bf16[64,16,512]{2,1,0:T(8,128)(2,1)S(1)} async-done(((bf16[64,16,512]{2,1,0:T(8,128)(2,1)}), bf16[64,16,512]{2,1,0:T(8,128)(2,1)S(1)}, u32[]{:S(2)}, u32[]{:S(2)}) %all-to-all-start) | async-done | bytes 1048608 | tf_op jit(solution)/shard_map/all_to_all | solution.py:101
  61.7 6.4 %all-to-all-start.2 = ((bf16[64,16,512]{2,1,0:T(8,128)(2,1)}), bf16[64,16,512]{2,1,0:T(8,128)(2,1)}, u32[]{:S(2)}, u32[]{:S(2)}) async-start(bf16[64,16,512]{2,1,0:T(8,128)(2,1)} %bitcast.126), calls=%async_computation.2 | async-start | bytes 2097152 | tf_op jit(solution)/shard_map/all_to_all | solution.py:101
  68.1 2.8 %fusion.44 = f32[512,2048]{1,0:T(8,128)S(1)} fusion(bf16[1,512,2048]{2,1,0:T(8,128)(2,1)} %param.18, bf16[64,16,512]{2,1,0:T(8,128)(2,1)S(1)} %all-to-all-done), kind=kOutput, calls=%fused_computation.52 | convolution fusion | flops 1073741824 | bytes 6815744 | tf_op jit(solution)/shard_map/dot_general | solution.py:36
  71.0 3.3 %fusion.6 = bf16[512,2048]{1,0:T(8,128)(2,1)S(1)} fusion(f32[512,2048]{1,0:T(8,128)S(1)} %fusion.44, bf16[1,2048,512]{2,1,0:T(8,128)(2,1)S(1)} %copy-done, bf16[64,16,512]{2,1,0:T(8,128)(2,1)S(1)} %all-to-all-done), kind=kOutput, calls=%fused_computation.10 | convolution fusion | flops 1093664768 | bytes 8912896 | tf_op jit(solution)/shard_map/dot_general | solution.py:30
  74.3 1.3 fusion.76
  75.6 1.4 fusion.70
  78.2 3.3 %fusion.85 = f32[512,2048]{1,0:T(8,128)} fusion(bf16[512,2048]{1,0:T(8,128)(2,1)S(1)} %fusion.6, bf16[64,16,512]{2,1,0:T(8,128)(2,1)S(1)} %all-to-all-done), kind=kOutput, calls=%fused_computation.102 | convolution fusion | flops 1073741824 | bytes 6815744 | tf_op jit(solution)/shard_map/dot_general | solution.py:24
  81.4 3.8 %fusion.86 = f32[2048,512]{1,0:T(8,128)} fusion(bf16[64,16,512]{2,1,0:T(8,128)(2,1)S(1)} %all-to-all-done, f32[512,2048]{1,0:T(8,128)S(1)} %fusion.44), kind=kOutput, calls=%fused_computation.103 | convolution fusion | flops 1083179008 | bytes 8912896 | tf_op jit(solution)/shard_map/dot_general | solution.py:24
  85.2 11.4 %all-to-all-done.2 = bf16[64,16,512]{2,1,0:T(8,128)(2,1)} async-done(((bf16[64,16,512]{2,1,0:T(8,128)(2,1)}), bf16[64,16,512]{2,1,0:T(8,128)(2,1)}, u32[]{:S(2)}, u32[]{:S(2)}) %all-to-all-start.2) | async-done | bytes 1048608 | tf_op jit(solution)/shard_map/all_to_all | solution.py:101
  96.5 6.4 %all-to-all-start.1 = ((bf16[64,16,512]{2,1,0:T(8,128)(2,1)}), bf16[64,16,512]{2,1,0:T(8,128)(2,1)}, u32[]{:S(2)}, u32[]{:S(2)}) async-start(bf16[64,16,512]{2,1,0:T(8,128)(2,1)} %pad_maximum_fusion), calls=%async_computation.1 | async-start | bytes 2097152 | tf_op jit(solution)/shard_map/all_to_all | solution.py:116
  103.2 3.0 %fusion.40 = f32[512,2048]{1,0:T(8,128)S(1)} fusion(bf16[1,512,2048]{2,1,0:T(8,128)(2,1)} %param.18, bf16[64,16,512]{2,1,0:T(8,128)(2,1)} %all-to-all-done.2), kind=kOutput, calls=%fused_computation.48 | convolution fusion | flops 1073741824 | bytes 6815744 | tf_op jit(solution)/shard_map/dot_general | solution.py:36
  106.3 4.9 %fusion.13 = bf16[512,2048]{1,0:T(8,128)(2,1)S(1)} fusion(f32[512,2048]{1,0:T(8,128)S(1)} %fusion.40, bf16[1,2048,512]{2,1,0:T(8,128)(2,1)S(1)} %copy-done, bf16[64,16,512]{2,1,0:T(8,128)(2,1)} %all-to-all-done.2), kind=kOutput, calls=%fused_computation.17 | convolution fusion | flops 1093664768 | bytes 8912896 | tf_op jit(solution)/shard_map/dot_general | solution.py:30
  111.2 4.2 %fusion.30 = bf16[1,512,2048]{2,1,0:T(8,128)(2,1)} fusion(f32[512,2048]{1,0:T(8,128)S(1)} %copy-done.3, bf16[512,2048]{1,0:T(8,128)(2,1)S(1)} %fusion.13, bf16[64,16,512]{2,1,0:T(8,128)(2,1)} %all-to-all-done.2), kind=kOutput, calls=%fused_computation.38 | convolution fusion | flops 1075838976 | bytes 8912896 | tf_op jit(solution)/shard_map/dot_general | solution.py:24
  115.4 4.1 %fusion.31 = bf16[1,2048,512]{2,1,0:T(8,128)(2,1)} fusion(f32[2048,512]{1,0:T(8,128)S(1)} %copy-done.13, bf16[64,16,512]{2,1,0:T(8,128)(2,1)} %all-to-all-done.2, f32[512,2048]{1,0:T(8,128)S(1)} %fusion.40), kind=kOutput, calls=%fused_computation.39 | convolution fusion | flops 1085276160 | bytes 11010048 | tf_op jit(solution)/shard_map/dot_general | solution.py:24
  119.5 3.8 %fusion.67 = bf16[64,8,512]{2,1,0:T(8,128)(2,1)S(1)} fusion(bf16[1,2048,512]{2,1,0:T(8,128)(2,1)S(1)} %copy-done, f32[512,2048]{1,0:T(8,128)} %copy-done.4), kind=kOutput, calls=%fused_computation.65 | convolution fusion | flops 1083441152 | bytes 6815744 | tf_op jit(solution)/shard_map/dot_general | solution.py:39
  123.3 1.3 fusion.73
  125.7 5.7 %all-to-all-done.1 = bf16[64,16,512]{2,1,0:T(8,128)(2,1)} async-done(((bf16[64,16,512]{2,1,0:T(8,128)(2,1)}), bf16[64,16,512]{2,1,0:T(8,128)(2,1)}, u32[]{:S(2)}, u32[]{:S(2)}) %all-to-all-start.1) | async-done | bytes 1048608 | tf_op jit(solution)/shard_map/all_to_all | solution.py:116
  131.4 6.4 %all-to-all-start.3 = ((bf16[64,16,512]{2,1,0:T(8,128)(2,1)}), bf16[64,16,512]{2,1,0:T(8,128)(2,1)}, u32[]{:S(2)}, u32[]{:S(2)}) async-start(bf16[64,16,512]{2,1,0:T(8,128)(2,1)} %pad_maximum_fusion.1), calls=%async_computation.3 | async-start | bytes 2097152 | tf_op jit(solution)/shard_map/all_to_all | solution.py:116
  138.4 1.2 iota_compare_fusion.1
  139.9 3.3 %fusion.14 = f32[768,512]{1,0:T(8,128)} fusion(bf16[1024,512]{1,0:T(8,128)(2,1)} %bitcast.16, pred[256,1024]{1,0:T(32,128)(4,1)S(1)} %fusion.81, pred[512,1024]{1,0:T(32,128)(4,1)S(1)} %iota_compare_fusion.3), kind=kOutput, calls=%fused_computation.22 | convolution fusion | flops 806092800 | bytes 3407872 | tf_op jit(solution)/shard_map/dot_general | solution.py:124
  143.3 22.9 %all-to-all-done.3 = bf16[64,16,512]{2,1,0:T(8,128)(2,1)} async-done(((bf16[64,16,512]{2,1,0:T(8,128)(2,1)}), bf16[64,16,512]{2,1,0:T(8,128)(2,1)}, u32[]{:S(2)}, u32[]{:S(2)}) %all-to-all-start.3) | async-done | bytes 1048608 | tf_op jit(solution)/shard_map/all_to_all | solution.py:116
  166.2 2.9 %fusion.49 = f32[768,512]{1,0:T(8,128)S(1)} fusion(f32[768,512]{1,0:T(8,128)} %fusion.14, bf16[1024,512]{1,0:T(8,128)(2,1)} %bitcast.28, pred[256,1024]{1,0:T(32,128)(4,1)S(1)} %fusion.83, pred[512,1024]{1,0:T(32,128)(4,1)} %iota_compare_fusion.1), kind=kOutput, calls=%fused_computation.59 | convolution fusion | flops 806486016 | bytes 4980736 | tf_op jit(solution)/shard_map/dot_general | solution.py:124
  170.3 1.1 fusion.80
  171.5 46.8 %all-reduce.3.cloned.1.call-done = (bf16[1,512,2048]{2,1,0:T(8,128)(2,1)}, bf16[1,2048,512]{2,1,0:T(8,128)(2,1)}) async-done(((bf16[1,512,2048]{2,1,0:T(8,128)(2,1)}, bf16[1,2048,512]{2,1,0:T(8,128)(2,1)}), (bf16[1,512,2048]{2,1,0:T(8,128)(2,1)}, bf16[1,2048,512]{2,1,0:T(8,128)(2,1)})) %all-reduce.3.cloned.1.call-update) | async-done | bytes 4194320 | tf_op jit(solution)/shard_map/psum | solution.py:126
  218.3 3.3 %copy.95 = bf16[1,512,2048]{2,1,0:T(8,128)(2,1)} copy(bf16[1,512,2048]{2,1,0:T(8,128)(2,1)} %get-tuple-element.36) | data formatting | bytes 4194304
  221.6 1.3 copy.96
  (71 shorter events, 12.3 us)
Async XLA Ops:
  7.2 63.8 %copy-start = (bf16[1,2048,512]{2,1,0:T(8,128)(2,1)S(1)}, bf16[1,2048,512]{2,1,0:T(8,128)(2,1)}, u32[]{:S(2)}) copy-start(bf16[1,2048,512]{2,1,0:T(8,128)(2,1)} %param.19) | copy-start | bytes 6291460
  18.0 2.0 copy-start.7
  18.1 2.0 copy-start.8
  20.0 41.7 %all-to-all-start = ((bf16[64,16,512]{2,1,0:T(8,128)(2,1)}), bf16[64,16,512]{2,1,0:T(8,128)(2,1)S(1)}, u32[]{:S(2)}, u32[]{:S(2)}) async-start(bf16[64,16,512]{2,1,0:T(8,128)(2,1)} %bitcast.127), calls=%async_computation | async-start | bytes 2097152 | tf_op jit(solution)/shard_map/all_to_all | solution.py:101
  61.7 34.8 %all-to-all-start.2 = ((bf16[64,16,512]{2,1,0:T(8,128)(2,1)}), bf16[64,16,512]{2,1,0:T(8,128)(2,1)}, u32[]{:S(2)}, u32[]{:S(2)}) async-start(bf16[64,16,512]{2,1,0:T(8,128)(2,1)} %bitcast.126), calls=%async_computation.2 | async-start | bytes 2097152 | tf_op jit(solution)/shard_map/all_to_all | solution.py:101
  71.0 3.3 %copy-start.1 = (bf16[1,512,2048]{2,1,0:T(8,128)(2,1)S(1)}, bf16[1,512,2048]{2,1,0:T(8,128)(2,1)}, u32[]{:S(2)}) copy-start(bf16[1,512,2048]{2,1,0:T(8,128)(2,1)} %param.18) | copy-start | bytes 6291460
  96.5 34.8 %all-to-all-start.1 = ((bf16[64,16,512]{2,1,0:T(8,128)(2,1)}), bf16[64,16,512]{2,1,0:T(8,128)(2,1)}, u32[]{:S(2)}, u32[]{:S(2)}) async-start(bf16[64,16,512]{2,1,0:T(8,128)(2,1)} %pad_maximum_fusion), calls=%async_computation.1 | async-start | bytes 2097152 | tf_op jit(solution)/shard_map/all_to_all | solution.py:116
  102.9 115.3 %all-reduce.3.cloned.1.call-start = ((), (), s32[]{:S(2)}) async-start(), calls=%async_computation.4 | async-start | bytes 8388608 | tf_op jit(solution)/shard_map/psum | solution.py:126
  106.2 9.1 %copy-start.4 = (f32[512,2048]{1,0:T(8,128)}, f32[512,2048]{1,0:T(8,128)S(1)}, u32[]{:S(2)}) copy-start(f32[512,2048]{1,0:T(8,128)S(1)} %fusion.40) | copy-start | bytes 12582916
  106.3 4.9 %copy-start.3 = (f32[512,2048]{1,0:T(8,128)S(1)}, f32[512,2048]{1,0:T(8,128)}, u32[]{:S(2)}) copy-start(f32[512,2048]{1,0:T(8,128)} %fusion.85) | copy-start | bytes 12582916
  111.1 4.2 %copy-start.11 = (bf16[512,2048]{1,0:T(8,128)(2,1)}, bf16[512,2048]{1,0:T(8,128)(2,1)S(1)}, u32[]{:S(2)}) copy-start(bf16[512,2048]{1,0:T(8,128)(2,1)S(1)} %fusion.13) | copy-start | bytes 6291460
  111.2 4.2 %copy-start.13 = (f32[2048,512]{1,0:T(8,128)S(1)}, f32[2048,512]{1,0:T(8,128)}, u32[]{:S(2)}) copy-start(f32[2048,512]{1,0:T(8,128)} %fusion.86) | copy-start | bytes 12582916
  119.5 3.8 %copy-start.2 = (bf16[1,512,2048]{2,1,0:T(8,128)(2,1)S(1)}, bf16[1,512,2048]{2,1,0:T(8,128)(2,1)}, u32[]{:S(2)}) copy-start(bf16[1,512,2048]{2,1,0:T(8,128)(2,1)} %param.18) | copy-start | bytes 6291460
  119.5 3.8 %copy-start.12 = (bf16[512,2048]{1,0:T(8,128)(2,1)S(1)}, bf16[512,2048]{1,0:T(8,128)(2,1)}, u32[]{:S(2)}) copy-start(bf16[512,2048]{1,0:T(8,128)(2,1)} %copy-done.11) | copy-start | bytes 6291460
  124.6 13.2 %copy-start.5 = (bf16[256,512]{1,0:T(8,128)(2,1)S(1)}, bf16[256,512]{1,0:T(8,128)(2,1)}, u32[]{:S(2)}) copy-start(bf16[256,512]{1,0:T(8,128)(2,1)} %param.13) | copy-start | bytes 786436
  131.4 34.8 %all-to-all-start.3 = ((bf16[64,16,512]{2,1,0:T(8,128)(2,1)}), bf16[64,16,512]{2,1,0:T(8,128)(2,1)}, u32[]{:S(2)}, u32[]{:S(2)}) async-start(bf16[64,16,512]{2,1,0:T(8,128)(2,1)} %pad_maximum_fusion.1), calls=%async_computation.3 | async-start | bytes 2097152 | tf_op jit(solution)/shard_map/all_to_all | solution.py:116
  166.2 3.3 %copy-start.10 = (s32[256,2]{0,1:T(2,128)S(1)}, s32[256,2]{0,1:T(2,128)}, u32[]{:S(2)}) copy-start(s32[256,2]{0,1:T(2,128)} %param.12) | copy-start | bytes 6148
  166.2 4.1 %copy-start.9 = (bf16[512,64]{0,1:T(8,128)(2,1)S(1)}, bf16[512,64]{0,1:T(8,128)(2,1)}, u32[]{:S(2)}) copy-start(bf16[512,64]{0,1:T(8,128)(2,1)} %param.17) | copy-start | bytes 196612
  218.3 3.3 %copy-start.6 = (bf16[1,2048,512]{2,1,0:T(8,128)(2,1)S(1)}, bf16[1,2048,512]{2,1,0:T(8,128)(2,1)}, u32[]{:S(2)}) copy-start(bf16[1,2048,512]{2,1,0:T(8,128)(2,1)} %get-tuple-element.37) | copy-start | bytes 6291460
Sparse Core Ops, SparseCore 0:
  119.6 98.6 all-reduce.2

commit v4 on v3

--- a/solution.py
+++ b/solution.py
@@ -49,7 +49,7 @@
     return (d_inputs, grad_up_part, grad_down_part)
 
 
-def per_device(
+def layer_body(
     features, slots, routes, cotangent, pos_table, tower_in, tower_out, router, w_up, w_down
 ):
     tok_rows = features.shape[0]
@@ -74,7 +74,6 @@
     slot_cot = jnp.concatenate(
         [(gates[:, k:k + 1] * cot_wide).astype(jnp.bfloat16) for k in range(TOP)]
     )
-    flat_routes = routes.reshape(-1)
     flat_hot = route_hot.reshape(-1, n_experts).astype(jnp.int32)
     before = jnp.cumsum(flat_hot, axis=0, dtype=jnp.int32) - flat_hot
     slot_rank = jnp.sum(before * flat_hot, axis=1, dtype=jnp.int32).reshape(tok_rows, TOP)
@@ -84,12 +83,15 @@
     w_down_one = w_down[0]
     spots = jnp.arange(n_experts * 2 * half, dtype=jnp.int32)
     gathered = []
+    backs = []
+    spots_of = []
     grad_ups = []
     grad_downs = []
     for chunk in range(2):
         mine = slot_rank // half == chunk
         in_spot = jnp.where(mine, routes * (2 * half) + slot_rank % half, -1)
         cot_spot = jnp.where(mine, in_spot + half, -1)
+        spots_of.append((in_spot, cot_spot))
         pick = jnp.concatenate(
             [
                 (spots[:, None] == in_spot[None, :, 0]) | (spots[:, None] == in_spot[None, :, 1]),
@@ -113,7 +115,16 @@
             [outputs.reshape(n_experts, half, feature_width), d_inputs.reshape(n_experts, half, feature_width)],
             axis=1,
         )
-        back = lax.all_to_all(back, "expert", split_axis=0, concat_axis=0, tiled=True)
+        backs.append(back)
+    part_up = (grad_ups[0] + grad_ups[1]).astype(jnp.bfloat16)[None]
+    part_down = (grad_downs[0] + grad_downs[1]).astype(jnp.bfloat16)[None]
+    first_back, part_up, part_down = lax.optimization_barrier((backs[0], part_up, part_down))
+    sum_up = lax.psum(part_up, "dp")
+    sum_down = lax.psum(part_down, "dp")
+    backs[0] = first_back
+    for chunk in range(2):
+        in_spot, cot_spot = spots_of[chunk]
+        back = lax.all_to_all(backs[chunk], "expert", split_axis=0, concat_axis=0, tiled=True)
         take = jnp.concatenate(
             [
                 in_spot.T.reshape(-1, 1) == spots[None, :],
@@ -123,8 +134,6 @@
         gathered.append(
             jnp.dot(take, back.reshape(-1, feature_width), preferred_element_type=jnp.float32)
         )
-    sum_up = lax.psum((grad_ups[0] + grad_ups[1]).astype(jnp.bfloat16), "dp")
-    sum_down = lax.psum((grad_downs[0] + grad_downs[1]).astype(jnp.bfloat16), "dp")
     picked = gathered[0] + gathered[1]
     expert_wide = jnp.stack([picked[k * tok_rows:(k + 1) * tok_rows] for k in range(TOP)], axis=1)
     grad_sum = picked[TOP * tok_rows:]
@@ -145,14 +154,18 @@
     return (
         layer_out,
         grad_in,
-        sum_up.astype(jnp.bfloat16)[None],
-        sum_down.astype(jnp.bfloat16)[None],
+        sum_up,
+        sum_down,
     )
 
 
 def solution(mesh):
+    return shard_map_of(mesh)
+
+
+def shard_map_of(mesh):
     return jax.shard_map(
-        per_device,
+        layer_body,
         mesh=mesh,
         in_specs=(
             P(("dp", "expert"), None),

time: 231 us -> 234 us (1.013)
  waiting for transfers between devices: 112 us -> 115 us
    all_to_all x4, waiting for transfers between devices: 64.9 us -> 80.6 us  [the longest x2 44.4 us: layer_body(): lax.all_to_all(backs[chunk], 'expert', split_axis=0, concat_axis=0, tiled...]
    psum x1, waiting for transfers between devices: 46.8 us -> 33.8 us  [layer_body(): sum_up = lax.psum(part_up, 'dp')]
  transfers between devices with their start and end apart: 5 -> 5, of which waited for: 5 -> 5; matrix products, arithmetic and copies ran while one was open for 23% -> 16% of each run, Pallas kernels for 0% -> 0%
where the time goes in v4:
time: 234 us; the launch traced here: 233 us
  waiting for transfers between devices  115 us (49%)
  matrix products  54 us (23%)
  starting transfers between devices  32.4 us (14%)
  between operations  14.5 us (6%)
  other arithmetic  10.6 us (5%)
  local copies, waits for them, and re-layouts  6.5 us (3%)
    all_to_all x2, waiting for transfers between devices, layer_body(): lax.all_to_all(backs[chunk], 'expert', split_axis=0, concat_axis=0, tiled...  44.4 us
    all_to_all x2, waiting for transfers between devices, layer_body(): lax.all_to_all(sent.reshape(n_experts, 2 * half, feature_width), 'expert'...  36.2 us
    psum x1, waiting for transfers between devices, layer_body(): sum_up = lax.psum(part_up, 'dp')  33.8 us
    all_to_all x2, starting transfers between devices, layer_body(): lax.all_to_all(sent.reshape(n_experts, 2 * half, feature_width), 'expert'...  19.5 us
    dot_general x4, matrix products, contract_rows(): lax.dot_general(left, right, (((0,), (0,)), ((), ())), preferred_element_...  15.3 us
    all_to_all x2, starting transfers between devices, layer_body(): lax.all_to_all(backs[chunk], 'expert', split_axis=0, concat_axis=0, tiled...  12.8 us
    dot_general x4, matrix products, contract_cols(): lax.dot_general(left, right, (((1,), (1,)), ((), ())), preferred_element_...  10.7 us
    dot_general x2, matrix products, layer_body(): jnp.dot(take, back.reshape(-1, feature_width), preferred_element_type=jnp...  6.39 us
  transfers between devices with their start and end apart: 5, of which 5 were waited for; matrix products, arithmetic and copies ran while one was open for 16% of the time, Pallas kernels for 0%

profile of v4, /device:TPU:1, one launch (start us, length us, event | category | flops | bytes accessed | tf_op | source)
XLA Modules:
  0.0 233.1 jit_solution(14751062374111699728)
XLA Ops:
  8.5 1.2 reduce-window.6
  11.9 1.2 fusion.107
  13.1 1.4 fusion.79
  18.1 2.0 fusion.52
  20.0 13.1 %all-to-all-start = ((bf16[64,16,512]{2,1,0:T(8,128)(2,1)}), bf16[64,16,512]{2,1,0:T(8,128)(2,1)S(1)}, u32[]{:S(2)}, u32[]{:S(2)}) async-start(bf16[64,16,512]{2,1,0:T(8,128)(2,1)} %bitcast.127), calls=%async_computation | async-start | bytes 2097152 | tf_op jit(solution)/shard_map/all_to_all | solution.py:103
  33.8 3.0 %fusion.49 = bf16[1024,512]{1,0:T(8,128)(2,1)} fusion(pred[1024,512]{1,0:T(32,128)(4,1)S(1)} %iota_compare_fusion.1, pred[1024,256]{1,0:T(32,128)(4,1)S(1)} %fusion.83, bf16[256,512]{1,0:T(8,128)(2,1)} %copy-done.8, bf16[256,512]{1,0:T(8,128)(2,1)} %copy-done.7, bf16[256,512]{1,0:T(8,128)(2,1)S(1)} %fusion.79), kind=kOutput, calls=%fused_computation.59 | convolution fusion | flops 808976384 | bytes 2621440 | tf_op jit(solution)/shard_map/dot_general | solution.py:102
  36.8 24.9 %all-to-all-done = bf16[64,16,512]{2,1,0:T(8,128)(2,1)S(1)} async-done(((bf16[64,16,512]{2,1,0:T(8,128)(2,1)}), bf16[64,16,512]{2,1,0:T(8,128)(2,1)S(1)}, u32[]{:S(2)}, u32[]{:S(2)}) %all-to-all-start) | async-done | bytes 1048608 | tf_op jit(solution)/shard_map/all_to_all | solution.py:103
  61.7 6.4 %all-to-all-start.1 = ((bf16[64,16,512]{2,1,0:T(8,128)(2,1)}), bf16[64,16,512]{2,1,0:T(8,128)(2,1)}, u32[]{:S(2)}, u32[]{:S(2)}) async-start(bf16[64,16,512]{2,1,0:T(8,128)(2,1)} %bitcast.126), calls=%async_computation.1 | async-start | bytes 2097152 | tf_op jit(solution)/shard_map/all_to_all | solution.py:103
  68.1 2.8 %fusion.44 = f32[512,2048]{1,0:T(8,128)S(1)} fusion(bf16[1,512,2048]{2,1,0:T(8,128)(2,1)} %param.18, bf16[64,16,512]{2,1,0:T(8,128)(2,1)S(1)} %all-to-all-done), kind=kOutput, calls=%fused_computation.52 | convolution fusion | flops 1073741824 | bytes 6815744 | tf_op jit(solution)/shard_map/dot_general | solution.py:36
  71.0 3.3 %fusion.6 = bf16[512,2048]{1,0:T(8,128)(2,1)S(1)} fusion(f32[512,2048]{1,0:T(8,128)S(1)} %fusion.44, bf16[1,2048,512]{2,1,0:T(8,128)(2,1)S(1)} %copy-done, bf16[64,16,512]{2,1,0:T(8,128)(2,1)S(1)} %all-to-all-done), kind=kOutput, calls=%fused_computation.10 | convolution fusion | flops 1093664768 | bytes 8912896 | tf_op jit(solution)/shard_map/dot_general | solution.py:30
  74.3 1.3 fusion.76
  75.6 1.4 fusion.70
  77.0 1.2 pad_maximum_fusion
  78.2 3.3 %fusion.85 = f32[512,2048]{1,0:T(8,128)} fusion(bf16[512,2048]{1,0:T(8,128)(2,1)S(1)} %fusion.6, bf16[64,16,512]{2,1,0:T(8,128)(2,1)S(1)} %all-to-all-done), kind=kOutput, calls=%fused_computation.102 | convolution fusion | flops 1073741824 | bytes 6815744 | tf_op jit(solution)/shard_map/dot_general | solution.py:24
  81.5 3.8 %fusion.86 = f32[2048,512]{1,0:T(8,128)} fusion(bf16[64,16,512]{2,1,0:T(8,128)(2,1)S(1)} %all-to-all-done, f32[512,2048]{1,0:T(8,128)S(1)} %fusion.44), kind=kOutput, calls=%fused_computation.103 | convolution fusion | flops 1083179008 | bytes 8912896 | tf_op jit(solution)/shard_map/dot_general | solution.py:24
  85.2 11.3 %all-to-all-done.1 = bf16[64,16,512]{2,1,0:T(8,128)(2,1)} async-done(((bf16[64,16,512]{2,1,0:T(8,128)(2,1)}), bf16[64,16,512]{2,1,0:T(8,128)(2,1)}, u32[]{:S(2)}, u32[]{:S(2)}) %all-to-all-start.1) | async-done | bytes 1048608 | tf_op jit(solution)/shard_map/all_to_all | solution.py:103
  96.5 3.0 %fusion.40 = f32[512,2048]{1,0:T(8,128)S(1)} fusion(bf16[1,512,2048]{2,1,0:T(8,128)(2,1)} %param.18, bf16[64,16,512]{2,1,0:T(8,128)(2,1)} %all-to-all-done.1), kind=kOutput, calls=%fused_computation.48 | convolution fusion | flops 1073741824 | bytes 6815744 | tf_op jit(solution)/shard_map/dot_general | solution.py:36
  99.6 4.9 %fusion.13 = bf16[512,2048]{1,0:T(8,128)(2,1)S(1)} fusion(f32[512,2048]{1,0:T(8,128)S(1)} %fusion.40, bf16[1,2048,512]{2,1,0:T(8,128)(2,1)S(1)} %copy-done, bf16[64,16,512]{2,1,0:T(8,128)(2,1)} %all-to-all-done.1), kind=kOutput, calls=%fused_computation.17 | convolution fusion | flops 1093664768 | bytes 8912896 | tf_op jit(solution)/shard_map/dot_general | solution.py:30
  104.5 4.6 %fusion.31 = bf16[1,2048,512]{2,1,0:T(8,128)(2,1)} fusion(f32[2048,512]{1,0:T(8,128)S(1)} %copy-done.13, bf16[64,16,512]{2,1,0:T(8,128)(2,1)} %all-to-all-done.1, f32[512,2048]{1,0:T(8,128)S(1)} %fusion.40), kind=kOutput, calls=%fused_computation.39 | convolution fusion | flops 1085276160 | bytes 11010048 | tf_op jit(solution)/shard_map/dot_general | solution.py:24
  109.1 3.6 %fusion.30 = bf16[1,512,2048]{2,1,0:T(8,128)(2,1)} fusion(f32[512,2048]{1,0:T(8,128)S(1)} %copy-done.4, bf16[512,2048]{1,0:T(8,128)(2,1)S(1)} %fusion.13, bf16[64,16,512]{2,1,0:T(8,128)(2,1)} %all-to-all-done.1), kind=kOutput, calls=%fused_computation.38 | convolution fusion | flops 1075838976 | bytes 8912896 | tf_op jit(solution)/shard_map/dot_general | solution.py:24
  112.7 6.4 %all-to-all-start.2 = ((bf16[64,16,512]{2,1,0:T(8,128)(2,1)}), bf16[64,16,512]{2,1,0:T(8,128)(2,1)}, u32[]{:S(2)}, u32[]{:S(2)}) async-start(bf16[64,16,512]{2,1,0:T(8,128)(2,1)} %pad_maximum_fusion), calls=%async_computation.2 | async-start | bytes 2097152 | tf_op jit(solution)/shard_map/all_to_all | solution.py:127
  119.9 3.8 %fusion.67 = bf16[64,8,512]{2,1,0:T(8,128)(2,1)S(1)} fusion(bf16[1,2048,512]{2,1,0:T(8,128)(2,1)S(1)} %copy-done, f32[512,2048]{1,0:T(8,128)} %copy-done.3), kind=kOutput, calls=%fused_computation.65 | convolution fusion | flops 1083441152 | bytes 6815744 | tf_op jit(solution)/shard_map/dot_general | solution.py:39
  123.7 1.3 fusion.73
  126.1 21.4 %all-to-all-done.2 = bf16[64,16,512]{2,1,0:T(8,128)(2,1)} async-done(((bf16[64,16,512]{2,1,0:T(8,128)(2,1)}), bf16[64,16,512]{2,1,0:T(8,128)(2,1)}, u32[]{:S(2)}, u32[]{:S(2)}) %all-to-all-start.2) | async-done | bytes 1048608 | tf_op jit(solution)/shard_map/all_to_all | solution.py:127
  147.6 6.4 %all-to-all-start.3 = ((bf16[64,16,512]{2,1,0:T(8,128)(2,1)}), bf16[64,16,512]{2,1,0:T(8,128)(2,1)}, u32[]{:S(2)}, u32[]{:S(2)}) async-start(bf16[64,16,512]{2,1,0:T(8,128)(2,1)} %pad_maximum_fusion.1), calls=%async_computation.3 | async-start | bytes 2097152 | tf_op jit(solution)/shard_map/all_to_all | solution.py:127
  154.6 1.2 iota_compare_fusion
  156.1 3.3 %fusion.14 = f32[768,512]{1,0:T(8,128)} fusion(bf16[1024,512]{1,0:T(8,128)(2,1)} %bitcast.24, pred[256,1024]{1,0:T(32,128)(4,1)S(1)} %fusion.81, pred[512,1024]{1,0:T(32,128)(4,1)S(1)} %iota_compare_fusion.3), kind=kOutput, calls=%fused_computation.22 | convolution fusion | flops 806092800 | bytes 3407872 | tf_op jit(solution)/shard_map/dot_general | solution.py:135
  159.5 22.9 %all-to-all-done.3 = bf16[64,16,512]{2,1,0:T(8,128)(2,1)} async-done(((bf16[64,16,512]{2,1,0:T(8,128)(2,1)}), bf16[64,16,512]{2,1,0:T(8,128)(2,1)}, u32[]{:S(2)}, u32[]{:S(2)}) %all-to-all-start.3) | async-done | bytes 1048608 | tf_op jit(solution)/shard_map/all_to_all | solution.py:127
  182.4 3.0 %fusion.46 = f32[768,512]{1,0:T(8,128)S(1)} fusion(f32[768,512]{1,0:T(8,128)} %fusion.14, bf16[1024,512]{1,0:T(8,128)(2,1)} %bitcast.30, pred[256,1024]{1,0:T(32,128)(4,1)S(1)} %fusion.84, pred[512,1024]{1,0:T(32,128)(4,1)} %iota_compare_fusion), kind=kOutput, calls=%fused_computation.58 | convolution fusion | flops 806486016 | bytes 4980736 | tf_op jit(solution)/shard_map/dot_general | solution.py:135
  187.8 33.8 %all-reduce.3.cloned.1.call-done = (bf16[1,512,2048]{2,1,0:T(8,128)(2,1)}, bf16[1,2048,512]{2,1,0:T(8,128)(2,1)}) async-done(((bf16[1,512,2048]{2,1,0:T(8,128)(2,1)}, bf16[1,2048,512]{2,1,0:T(8,128)(2,1)}), (bf16[1,512,2048]{2,1,0:T(8,128)(2,1)}, bf16[1,2048,512]{2,1,0:T(8,128)(2,1)})) %all-reduce.3.cloned.1.call-update) | async-done | bytes 4194320 | tf_op jit(solution)/shard_map/psum | solution.py:122
  221.6 3.3 %copy.95 = bf16[1,512,2048]{2,1,0:T(8,128)(2,1)} copy(bf16[1,512,2048]{2,1,0:T(8,128)(2,1)} %get-tuple-element.42) | data formatting | bytes 4194304
  225.0 1.3 copy.96
  (71 shorter events, 12.7 us)
Async XLA Ops:
  7.2 63.8 %copy-start = (bf16[1,2048,512]{2,1,0:T(8,128)(2,1)S(1)}, bf16[1,2048,512]{2,1,0:T(8,128)(2,1)}, u32[]{:S(2)}) copy-start(bf16[1,2048,512]{2,1,0:T(8,128)(2,1)} %param.19) | copy-start | bytes 6291460
  18.0 2.0 copy-start.7
  18.1 2.0 copy-start.8
  20.0 41.7 %all-to-all-start = ((bf16[64,16,512]{2,1,0:T(8,128)(2,1)}), bf16[64,16,512]{2,1,0:T(8,128)(2,1)S(1)}, u32[]{:S(2)}, u32[]{:S(2)}) async-start(bf16[64,16,512]{2,1,0:T(8,128)(2,1)} %bitcast.127), calls=%async_computation | async-start | bytes 2097152 | tf_op jit(solution)/shard_map/all_to_all | solution.py:103
  61.7 34.8 %all-to-all-start.1 = ((bf16[64,16,512]{2,1,0:T(8,128)(2,1)}), bf16[64,16,512]{2,1,0:T(8,128)(2,1)}, u32[]{:S(2)}, u32[]{:S(2)}) async-start(bf16[64,16,512]{2,1,0:T(8,128)(2,1)} %bitcast.126), calls=%async_computation.1 | async-start | bytes 2097152 | tf_op jit(solution)/shard_map/all_to_all | solution.py:103
  71.0 3.3 %copy-start.1 = (bf16[1,512,2048]{2,1,0:T(8,128)(2,1)S(1)}, bf16[1,512,2048]{2,1,0:T(8,128)(2,1)}, u32[]{:S(2)}) copy-start(bf16[1,512,2048]{2,1,0:T(8,128)(2,1)} %param.18) | copy-start | bytes 6291460
  99.6 4.9 %copy-start.3 = (f32[512,2048]{1,0:T(8,128)}, f32[512,2048]{1,0:T(8,128)S(1)}, u32[]{:S(2)}) copy-start(f32[512,2048]{1,0:T(8,128)S(1)} %fusion.40) | copy-start | bytes 12582916
  99.6 4.9 %copy-start.13 = (f32[2048,512]{1,0:T(8,128)S(1)}, f32[2048,512]{1,0:T(8,128)}, u32[]{:S(2)}) copy-start(f32[2048,512]{1,0:T(8,128)} %fusion.86) | copy-start | bytes 12582916
  104.5 4.6 %copy-start.11 = (bf16[512,2048]{1,0:T(8,128)(2,1)}, bf16[512,2048]{1,0:T(8,128)(2,1)S(1)}, u32[]{:S(2)}) copy-start(bf16[512,2048]{1,0:T(8,128)(2,1)S(1)} %fusion.13) | copy-start | bytes 6291460
  104.5 4.6 %copy-start.4 = (f32[512,2048]{1,0:T(8,128)S(1)}, f32[512,2048]{1,0:T(8,128)}, u32[]{:S(2)}) copy-start(f32[512,2048]{1,0:T(8,128)} %fusion.85) | copy-start | bytes 12582916
  112.7 34.8 %all-to-all-start.2 = ((bf16[64,16,512]{2,1,0:T(8,128)(2,1)}), bf16[64,16,512]{2,1,0:T(8,128)(2,1)}, u32[]{:S(2)}, u32[]{:S(2)}) async-start(bf16[64,16,512]{2,1,0:T(8,128)(2,1)} %pad_maximum_fusion), calls=%async_computation.2 | async-start | bytes 2097152 | tf_op jit(solution)/shard_map/all_to_all | solution.py:127
  119.1 102.5 %all-reduce.3.cloned.1.call-start = ((), (), s32[]{:S(2)}) async-start(), calls=%async_computation.4 | async-start | bytes 8388608 | tf_op jit(solution)/shard_map/psum | solution.py:122
  119.9 3.8 %copy-start.2 = (bf16[1,512,2048]{2,1,0:T(8,128)(2,1)S(1)}, bf16[1,512,2048]{2,1,0:T(8,128)(2,1)}, u32[]{:S(2)}) copy-start(bf16[1,512,2048]{2,1,0:T(8,128)(2,1)} %param.18) | copy-start | bytes 6291460
  119.9 3.8 %copy-start.12 = (bf16[512,2048]{1,0:T(8,128)(2,1)S(1)}, bf16[512,2048]{1,0:T(8,128)(2,1)}, u32[]{:S(2)}) copy-start(bf16[512,2048]{1,0:T(8,128)(2,1)} %copy-done.11) | copy-start | bytes 6291460
  125.0 29.0 %copy-start.5 = (bf16[256,512]{1,0:T(8,128)(2,1)S(1)}, bf16[256,512]{1,0:T(8,128)(2,1)}, u32[]{:S(2)}) copy-start(bf16[256,512]{1,0:T(8,128)(2,1)} %param.13) | copy-start | bytes 786436
  147.6 34.8 %all-to-all-start.3 = ((bf16[64,16,512]{2,1,0:T(8,128)(2,1)}), bf16[64,16,512]{2,1,0:T(8,128)(2,1)}, u32[]{:S(2)}, u32[]{:S(2)}) async-start(bf16[64,16,512]{2,1,0:T(8,128)(2,1)} %pad_maximum_fusion.1), calls=%async_computation.3 | async-start | bytes 2097152 | tf_op jit(solution)/shard_map/all_to_all | solution.py:127
  182.4 3.5 %copy-start.10 = (s32[256,2]{0,1:T(2,128)S(1)}, s32[256,2]{0,1:T(2,128)}, u32[]{:S(2)}) copy-start(s32[256,2]{0,1:T(2,128)} %param.12) | copy-start | bytes 6148
  182.4 4.3 %copy-start.9 = (bf16[512,64]{0,1:T(8,128)(2,1)S(1)}, bf16[512,64]{0,1:T(8,128)(2,1)}, u32[]{:S(2)}) copy-start(bf16[512,64]{0,1:T(8,128)(2,1)} %param.17) | copy-start | bytes 196612
  221.6 3.3 %copy-start.6 = (bf16[1,2048,512]{2,1,0:T(8,128)(2,1)S(1)}, bf16[1,2048,512]{2,1,0:T(8,128)(2,1)}, u32[]{:S(2)}) copy-start(bf16[1,2048,512]{2,1,0:T(8,128)(2,1)} %get-tuple-element.43) | copy-start | bytes 6291460
Sparse Core Ops, SparseCore 0:
  123.0 98.6 all-reduce.2

commit v5 on v4

--- a/solution.py
+++ b/solution.py
@@ -74,24 +74,29 @@
     slot_cot = jnp.concatenate(
         [(gates[:, k:k + 1] * cot_wide).astype(jnp.bfloat16) for k in range(TOP)]
     )
-    flat_hot = route_hot.reshape(-1, n_experts).astype(jnp.int32)
-    before = jnp.cumsum(flat_hot, axis=0, dtype=jnp.int32) - flat_hot
-    slot_rank = jnp.sum(before * flat_hot, axis=1, dtype=jnp.int32).reshape(tok_rows, TOP)
-    half = capacity // 2
+    flat_hot = jnp.concatenate([routes[:, k:k + 1] == expert_ids[None, :] for k in range(TOP)])
+    order = jnp.arange(TOP * tok_rows, dtype=jnp.int32)
+    earlier = (order[None, :] < order[:, None]).astype(jnp.bfloat16)
+    before = jnp.dot(earlier, flat_hot.astype(jnp.bfloat16), preferred_element_type=jnp.float32)
+    slot_rank = jnp.sum(jnp.where(flat_hot, before, 0.0), axis=1).astype(jnp.int32)
+    slot_rank = slot_rank.reshape(TOP, tok_rows).T
+    first_size = (5 * capacity) // 8
+    bounds = ((0, first_size), (first_size, capacity - first_size))
     rows_in = jnp.concatenate([mixed_in, slot_cot])
     w_up_one = w_up[0]
     w_down_one = w_down[0]
-    spots = jnp.arange(n_experts * 2 * half, dtype=jnp.int32)
     gathered = []
     backs = []
     spots_of = []
     grad_ups = []
     grad_downs = []
     for chunk in range(2):
-        mine = slot_rank // half == chunk
-        in_spot = jnp.where(mine, routes * (2 * half) + slot_rank % half, -1)
+        low, half = bounds[chunk]
+        spots = jnp.arange(n_experts * 2 * half, dtype=jnp.int32)
+        mine = (slot_rank >= low) & (slot_rank < low + half)
+        in_spot = jnp.where(mine, routes * (2 * half) + slot_rank - low, -1)
         cot_spot = jnp.where(mine, in_spot + half, -1)
-        spots_of.append((in_spot, cot_spot))
+        spots_of.append((in_spot, cot_spot, spots))
         pick = jnp.concatenate(
             [
                 (spots[:, None] == in_spot[None, :, 0]) | (spots[:, None] == in_spot[None, :, 1]),
@@ -123,7 +128,7 @@
     sum_down = lax.psum(part_down, "dp")
     backs[0] = first_back
     for chunk in range(2):
-        in_spot, cot_spot = spots_of[chunk]
+        in_spot, cot_spot, spots = spots_of[chunk]
         back = lax.all_to_all(backs[chunk], "expert", split_axis=0, concat_axis=0, tiled=True)
         take = jnp.concatenate(
             [

time: 234 us -> 280 us (1.20)
  local copies, waits for them, and re-layouts: 6.5 us -> 29.1 us
  waiting for transfers between devices: 115 us -> 133 us
  starting transfers between devices: 32.4 us -> 36.5 us
    psum x1, waiting for transfers between devices: 33.8 us -> 54.9 us  [layer_body(): sum_up = lax.psum(part_up, 'dp')]
    reshape x2 -> x12, local copies, waits for them, and re-layouts: 0.22 us -> 16.6 us  [the longest x2 4.32 us: layer_body(): sent.reshape(n_experts, 2 * half, feature_width)]
    all_to_all x2, waiting for transfers between devices: 44.4 us -> 34 us  [layer_body(): lax.all_to_all(backs[chunk], 'expert', split_axis=0, concat_axis=0, tiled...]
    all_to_all x2, waiting for transfers between devices: 36.2 us -> 43.5 us  [layer_body(): lax.all_to_all(sent.reshape(n_experts, 2 * half, feature_width), 'expert'...]
    slice x1 -> x5, local copies, waits for them, and re-layouts: 0.23 us -> 5.31 us  [the longest x2 4.45 us: layer_body(): flat_cot = recv[:, half:].reshape(-1, feature_width)]
    all_to_all x2, starting transfers between devices: 12.8 us -> 16.9 us  [layer_body(): lax.all_to_all(backs[chunk], 'expert', split_axis=0, concat_axis=0, tiled...]
    dot_general x2, matrix products: 5.24 us -> 9.03 us  [expert_forward(): jnp.dot(hidden, w_down_one, preferred_element_type=jnp.float32)]
    dot_general x4, matrix products: 15.3 us -> 12.1 us  [contract_rows(): lax.dot_general(left, right, (((0,), (0,)), ((), ())), preferred_element_...]
  transfers between devices with their start and end apart: 5 -> 5, of which waited for: 5 -> 4; matrix products, arithmetic and copies ran while one was open for 16% -> 27% of each run, Pallas kernels for 0% -> 0%
where the time goes in v5:
time: 280 us; the launch traced here: 279 us
  waiting for transfers between devices  133 us (48%)
  matrix products  53.2 us (19%)
  starting transfers between devices  36.5 us (13%)
  local copies, waits for them, and re-layouts  29.1 us (10%)
  between operations  14.7 us (5%)
  other arithmetic  12.1 us (4%)
    psum x1, waiting for transfers between devices, layer_body(): sum_up = lax.psum(part_up, 'dp')  54.9 us
    all_to_all x2, waiting for transfers between devices, layer_body(): lax.all_to_all(sent.reshape(n_experts, 2 * half, feature_width), 'expert'...  43.5 us
    all_to_all x2, waiting for transfers between devices, layer_body(): lax.all_to_all(backs[chunk], 'expert', split_axis=0, concat_axis=0, tiled...  34 us
    all_to_all x2, starting transfers between devices, layer_body(): lax.all_to_all(sent.reshape(n_experts, 2 * half, feature_width), 'expert'...  19.5 us
    all_to_all x2, starting transfers between devices, layer_body(): lax.all_to_all(backs[chunk], 'expert', split_axis=0, concat_axis=0, tiled...  16.9 us
    dot_general x4, matrix products, contract_rows(): lax.dot_general(left, right, (((0,), (0,)), ((), ())), preferred_element_...  12.1 us
    dot_general x4, matrix products, contract_cols(): lax.dot_general(left, right, (((1,), (1,)), ((), ())), preferred_element_...  10 us
    dot_general x2, matrix products, expert_forward(): jnp.dot(hidden, w_down_one, preferred_element_type=jnp.float32)  9.03 us
  transfers between devices with their start and end apart: 5, of which 4 were waited for; matrix products, arithmetic and copies ran while one was open for 27% of the time, Pallas kernels for 0%

profile of v5, /device:TPU:1, one launch (start us, length us, event | category | flops | bytes accessed | tf_op | source)
XLA Modules:
  0.0 278.7 jit_solution(8379906386920437079)
XLA Ops:
  11.2 1.4 fusion.69
  19.3 13.1 %all-to-all-start.1 = ((bf16[64,12,512]{2,1,0:T(8,128)(2,1)}), bf16[64,12,512]{2,1,0:T(8,128)(2,1)S(1)}, u32[]{:S(2)}, u32[]{:S(2)}) async-start(bf16[64,12,512]{2,1,0:T(8,128)(2,1)} %reshape.128), calls=%async_computation.1 | async-start | bytes 2097152 | tf_op jit(solution)/shard_map/all_to_all | solution.py:108
  33.2 3.3 %fusion.22 = bf16[1280,512]{1,0:T(8,128)(2,1)} fusion(pred[1280,512]{1,0:T(32,128)(4,1)S(1)} %iota_compare_fusion, pred[1280,256]{1,0:T(32,128)(4,1)S(1)} %fusion.62, bf16[256,512]{1,0:T(8,128)(2,1)} %copy-done.20, bf16[256,512]{1,0:T(8,128)(2,1)} %copy-done.19, bf16[256,512]{1,0:T(8,128)(2,1)S(1)} %fusion.69), kind=kOutput, calls=%fused_computation.30 | convolution fusion | flops 1010630656 | bytes 3080192 | tf_op jit(solution)/shard_map/dot_general | solution.py:107
  36.5 3.2 %reshape.123 = bf16[64,20,512]{2,1,0:T(8,128)(2,1)} reshape(bf16[1280,512]{1,0:T(8,128)(2,1)} %fusion.22) | data formatting | bytes 2621440 | tf_op jit(solution)/shard_map/reshape | solution.py:109
  39.7 21.2 %all-to-all-done.1 = bf16[64,12,512]{2,1,0:T(8,128)(2,1)S(1)} async-done(((bf16[64,12,512]{2,1,0:T(8,128)(2,1)}), bf16[64,12,512]{2,1,0:T(8,128)(2,1)S(1)}, u32[]{:S(2)}, u32[]{:S(2)}) %all-to-all-start.1) | async-done | bytes 786464 | tf_op jit(solution)/shard_map/all_to_all | solution.py:108
  60.9 6.4 %all-to-all-start = ((bf16[64,20,512]{2,1,0:T(8,128)(2,1)}), bf16[64,20,512]{2,1,0:T(8,128)(2,1)}, u32[]{:S(2)}, u32[]{:S(2)}) async-start(bf16[64,20,512]{2,1,0:T(8,128)(2,1)} %reshape.123), calls=%async_computation | async-start | bytes 3145728 | tf_op jit(solution)/shard_map/all_to_all | solution.py:108
  70.8 2.7 fusion.43
  73.6 2.6 fusion.21
  78.5 3.8 %fusion.66 = bf16[384,512]{1,0:T(8,128)(2,1)} fusion(bf16[1,2048,512]{2,1,0:T(8,128)(2,1)S(1)} %copy-done, f32[384,2048]{1,0:T(8,128)} %copy-done.6), kind=kOutput, calls=%fused_computation.71 | convolution fusion | flops 812580864 | bytes 5636096 | tf_op jit(solution)/shard_map/dot_general | solution.py:39
  83.3 1.4 pad_maximum_fusion.1
  84.7 22.3 %all-to-all-done = bf16[64,20,512]{2,1,0:T(8,128)(2,1)} async-done(((bf16[64,20,512]{2,1,0:T(8,128)(2,1)}), bf16[64,20,512]{2,1,0:T(8,128)(2,1)}, u32[]{:S(2)}, u32[]{:S(2)}) %all-to-all-start) | async-done | bytes 1310752 | tf_op jit(solution)/shard_map/all_to_all | solution.py:108
  107.0 6.5 %all-to-all-start.3 = ((bf16[64,12,512]{2,1,0:T(8,128)(2,1)}), bf16[64,12,512]{2,1,0:T(8,128)(2,1)}, u32[]{:S(2)}, u32[]{:S(2)}) async-start(bf16[64,12,512]{2,1,0:T(8,128)(2,1)} %pad_maximum_fusion.1), calls=%async_computation.3 | async-start | bytes 2097152 | tf_op jit(solution)/shard_map/all_to_all | solution.py:132
  113.5 3.3 %fusion.93 = (bf16[64,10,512]{2,1,0:T(8,128)(2,1)}, bf16[64,10,512]{2,1,0:T(8,128)(2,1)}) fusion(bf16[64,20,512]{2,1,0:T(8,128)(2,1)} %all-to-all-done), kind=kLoop, calls=%fused_computation.131 | loop fusion | bytes 2621440 | tf_op jit(solution)/shard_map/slice | solution.py:112
  116.8 1.4 reshape.124
  118.2 5.7 %fusion.47 = f32[640,2048]{1,0:T(8,128)} fusion(bf16[640,512]{1,0:T(8,128)(2,1)S(1)} %reshape.124, bf16[1,512,2048]{2,1,0:T(8,128)(2,1)} %param.18), kind=kOutput, calls=%fused_computation.55 | convolution fusion | flops 1342177280 | bytes 7995392 | tf_op jit(solution)/shard_map/dot_general | solution.py:36
  123.9 2.2 reshape.126
  126.1 5.3 %fusion.58 = bf16[640,512]{1,0:T(8,128)(2,1)} fusion(bf16[1,2048,512]{2,1,0:T(8,128)(2,1)S(1)} %copy-done, f32[640,2048]{1,0:T(8,128)} %fusion.47), kind=kOutput, calls=%fused_computation.63 | convolution fusion | flops 1354301440 | bytes 7995392 | tf_op jit(solution)/shard_map/dot_general | solution.py:39
  131.4 4.1 %fusion.6 = bf16[640,2048]{1,0:T(8,128)(2,1)S(1)} fusion(f32[640,2048]{1,0:T(8,128)S(1)} %bitcast.103, bf16[640,512]{1,0:T(8,128)(2,1)S(1)} %copy-done.15, bf16[1,2048,512]{2,1,0:T(8,128)(2,1)S(1)} %copy-done), kind=kOutput, calls=%fused_computation.8 | convolution fusion | flops 1367080960 | bytes 10616832 | tf_op jit(solution)/shard_map/dot_general | solution.py:30
  135.4 2.4 fusion.55
  137.9 1.8 fusion.103
  139.7 2.7 fusion.25
  142.4 1.3 reshape.127
  145.0 1.7 pad_maximum_fusion
  146.7 4.6 %fusion.89 = f32[2048,512]{1,0:T(8,128)S(1)} fusion(bf16[640,512]{1,0:T(8,128)(2,1)S(1)} %copy-done.16, f32[640,2048]{1,0:T(8,128)} %fusion.47), kind=kOutput, calls=%fused_computation.129 | convolution fusion | flops 1353973760 | bytes 10092544 | tf_op jit(solution)/shard_map/dot_general | solution.py:24
  151.3 3.0 %fusion.26 = bf16[1,2048,512]{2,1,0:T(8,128)(2,1)} fusion(f32[2048,512]{1,0:T(8,128)S(1)} %fusion.89, bf16[384,512]{1,0:T(8,128)(2,1)S(1)} %copy-done.18, f32[384,2048]{1,0:T(8,128)S(1)} %copy-done.7), kind=kOutput, calls=%fused_computation.32 | convolution fusion | flops 814481408 | bytes 9830400 | tf_op jit(solution)/shard_map/dot_general | solution.py:24
  154.3 10.5 %all-to-all-start.2 = ((bf16[64,20,512]{2,1,0:T(8,128)(2,1)}), bf16[64,20,512]{2,1,0:T(8,128)(2,1)S(1)}, u32[]{:S(2)}, u32[]{:S(2)}) async-start(bf16[64,20,512]{2,1,0:T(8,128)(2,1)} %pad_maximum_fusion), calls=%async_computation.2 | async-start | bytes 3145728 | tf_op jit(solution)/shard_map/all_to_all | solution.py:132
  169.2 1.3 reshape.134
  170.5 34.0 %all-to-all-done.2 = bf16[64,20,512]{2,1,0:T(8,128)(2,1)S(1)} async-done(((bf16[64,20,512]{2,1,0:T(8,128)(2,1)}), bf16[64,20,512]{2,1,0:T(8,128)(2,1)S(1)}, u32[]{:S(2)}, u32[]{:S(2)}) %all-to-all-start.2) | async-done | bytes 1310752 | tf_op jit(solution)/shard_map/all_to_all | solution.py:132
  205.7 2.8 %fusion.7 = f32[768,512]{1,0:T(8,128)S(1)} fusion(bf16[1280,512]{1,0:T(8,128)(2,1)} %reshape.131, pred[256,1280]{1,0:T(32,128)(4,1)} %fusion.61, pred[512,1280]{1,0:T(32,128)(4,1)} %iota_compare_fusion.1), kind=kOutput, calls=%fused_computation.14 | convolution fusion | flops 1007616000 | bytes 3866624 | tf_op jit(solution)/shard_map/dot_general | solution.py:140
  212.3 54.9 %all-reduce.3.cloned.1.call-done = (bf16[1,512,2048]{2,1,0:T(8,128)(2,1)}, bf16[1,2048,512]{2,1,0:T(8,128)(2,1)}) async-done(((bf16[1,512,2048]{2,1,0:T(8,128)(2,1)}, bf16[1,2048,512]{2,1,0:T(8,128)(2,1)}), (bf16[1,512,2048]{2,1,0:T(8,128)(2,1)}, bf16[1,2048,512]{2,1,0:T(8,128)(2,1)})) %all-reduce.3.cloned.1.call-update) | async-done | bytes 4194320 | tf_op jit(solution)/shard_map/psum | solution.py:127
  267.2 3.3 %copy.56 = bf16[1,512,2048]{2,1,0:T(8,128)(2,1)} copy(bf16[1,512,2048]{2,1,0:T(8,128)(2,1)} %get-tuple-element.46) | data formatting | bytes 4194304
  270.6 1.3 copy.57
  (117 shorter events, 28.8 us)
Async XLA Ops:
  7.2 66.4 %copy-start = (bf16[1,2048,512]{2,1,0:T(8,128)(2,1)S(1)}, bf16[1,2048,512]{2,1,0:T(8,128)(2,1)}, u32[]{:S(2)}) copy-start(bf16[1,2048,512]{2,1,0:T(8,128)(2,1)} %param.19) | copy-start | bytes 6291460
  9.1 23.4 %copy-start.23 = (s32[256,2]{0,1:T(2,128)}, s32[256,2]{0,1:T(2,128)S(1)}, u32[]{:S(2)}) copy-start(s32[256,2]{0,1:T(2,128)S(1)} %get-tuple-element.29) | copy-start | bytes 6148
  12.6 20.7 %copy-start.9 = (bf16[256,512]{1,0:T(8,128)(2,1)}, bf16[256,512]{1,0:T(8,128)(2,1)S(1)}, u32[]{:S(2)}) copy-start(bf16[256,512]{1,0:T(8,128)(2,1)S(1)} %fusion.69) | copy-start | bytes 786436
  15.0 3.1 %copy-start.27 = (f32[256]{0:T(256)}, f32[256]{0:T(256)S(1)}, u32[]{:S(2)}) copy-start(f32[256]{0:T(256)S(1)} %get-tuple-element.16) | copy-start | bytes 3076
  15.0 3.1 %copy-start.25 = (f32[256,2]{0,1:T(2,128)}, f32[256,2]{0,1:T(2,128)S(1)}, u32[]{:S(2)}) copy-start(f32[256,2]{0,1:T(2,128)S(1)} %multiply_divide_fusion) | copy-start | bytes 6148
  16.6 1.5 copy-start.19
  19.3 41.7 %all-to-all-start.1 = ((bf16[64,12,512]{2,1,0:T(8,128)(2,1)}), bf16[64,12,512]{2,1,0:T(8,128)(2,1)S(1)}, u32[]{:S(2)}, u32[]{:S(2)}) async-start(bf16[64,12,512]{2,1,0:T(8,128)(2,1)} %reshape.128), calls=%async_computation.1 | async-start | bytes 2097152 | tf_op jit(solution)/shard_map/all_to_all | solution.py:108
  60.9 46.1 %all-to-all-start = ((bf16[64,20,512]{2,1,0:T(8,128)(2,1)}), bf16[64,20,512]{2,1,0:T(8,128)(2,1)}, u32[]{:S(2)}, u32[]{:S(2)}) async-start(bf16[64,20,512]{2,1,0:T(8,128)(2,1)} %reshape.123), calls=%async_computation | async-start | bytes 3145728 | tf_op jit(solution)/shard_map/all_to_all | solution.py:108
  70.8 5.3 %copy-start.17 = (bf16[384,512]{1,0:T(8,128)(2,1)}, bf16[384,512]{1,0:T(8,128)(2,1)S(1)}, u32[]{:S(2)}) copy-start(bf16[384,512]{1,0:T(8,128)(2,1)S(1)} %reshape.130) | copy-start | bytes 1179652
  73.5 2.6 copy-start.6
  73.6 3.7 %copy-start.2 = (bf16[1,512,2048]{2,1,0:T(8,128)(2,1)S(1)}, bf16[1,512,2048]{2,1,0:T(8,128)(2,1)}, u32[]{:S(2)}) copy-start(bf16[1,512,2048]{2,1,0:T(8,128)(2,1)} %param.18) | copy-start | bytes 6291460
  76.2 1.1 copy-start.13
  107.0 47.2 %all-to-all-start.3 = ((bf16[64,12,512]{2,1,0:T(8,128)(2,1)}), bf16[64,12,512]{2,1,0:T(8,128)(2,1)}, u32[]{:S(2)}, u32[]{:S(2)}) async-start(bf16[64,12,512]{2,1,0:T(8,128)(2,1)} %pad_maximum_fusion.1), calls=%async_computation.3 | async-start | bytes 2097152 | tf_op jit(solution)/shard_map/all_to_all | solution.py:132
  118.2 5.7 %copy-start.4 = (bf16[640,512]{1,0:T(8,128)(2,1)}, bf16[640,512]{1,0:T(8,128)(2,1)S(1)}, u32[]{:S(2)}) copy-start(bf16[640,512]{1,0:T(8,128)(2,1)S(1)} %reshape.124) | copy-start | bytes 1966084
  123.9 7.5 %slice-start = ((s8[5242880]{0:T(1024)(128)(4,1)}), s8[1048576]{0:T(1024)(128)(4,1)S(1)}, s32[]{:S(2)}) async-start(s8[5242880]{0:T(1024)(128)(4,1)} %bitcast.102), calls=%async_computation.5 | async-start | bytes 2097152
  126.1 5.3 %slice-start.1 = ((s8[5242880]{0:T(1024)(128)(4,1)}), s8[4194304]{0:T(1024)(128)(4,1)S(1)}, s32[]{:S(2)}) async-start(s8[5242880]{0:T(1024)(128)(4,1)} %bitcast.102), calls=%async_computation.6 | async-start | bytes 8388608
  126.1 5.3 %copy-start.15 = (bf16[640,512]{1,0:T(8,128)(2,1)S(1)}, bf16[640,512]{1,0:T(8,128)(2,1)}, u32[]{:S(2)}) copy-start(bf16[640,512]{1,0:T(8,128)(2,1)} %reshape.126) | copy-start | bytes 1966084
  131.3 4.1 %copy-start.3 = (bf16[1,512,2048]{2,1,0:T(8,128)(2,1)S(1)}, bf16[1,512,2048]{2,1,0:T(8,128)(2,1)}, u32[]{:S(2)}) copy-start(bf16[1,512,2048]{2,1,0:T(8,128)(2,1)} %param.18) | copy-start | bytes 6291460
  135.4 2.4 copy-start.5
  137.9 1.9 copy-start.14
  142.4 4.3 %copy-start.16 = (bf16[640,512]{1,0:T(8,128)(2,1)S(1)}, bf16[640,512]{1,0:T(8,128)(2,1)}, u32[]{:S(2)}) copy-start(bf16[640,512]{1,0:T(8,128)(2,1)} %reshape.126) | copy-start | bytes 1966084
  146.7 4.6 %copy-start.7 = (f32[384,2048]{1,0:T(8,128)S(1)}, f32[384,2048]{1,0:T(8,128)}, u32[]{:S(2)}) copy-start(f32[384,2048]{1,0:T(8,128)} %copy-done.6) | copy-start | bytes 9437188
  146.7 4.6 %copy-start.18 = (bf16[384,512]{1,0:T(8,128)(2,1)S(1)}, bf16[384,512]{1,0:T(8,128)(2,1)}, u32[]{:S(2)}) copy-start(bf16[384,512]{1,0:T(8,128)(2,1)} %copy-done.17) | copy-start | bytes 1179652
  154.3 11.2 %copy-start.8 = (bf16[256,512]{1,0:T(8,128)(2,1)S(1)}, bf16[256,512]{1,0:T(8,128)(2,1)}, u32[]{:S(2)}) copy-start(bf16[256,512]{1,0:T(8,128)(2,1)} %param.13) | copy-start | bytes 786436
  154.3 50.2 %all-to-all-start.2 = ((bf16[64,20,512]{2,1,0:T(8,128)(2,1)}), bf16[64,20,512]{2,1,0:T(8,128)(2,1)S(1)}, u32[]{:S(2)}, u32[]{:S(2)}) async-start(bf16[64,20,512]{2,1,0:T(8,128)(2,1)} %pad_maximum_fusion), calls=%async_computation.2 | async-start | bytes 3145728 | tf_op jit(solution)/shard_map/all_to_all | solution.py:132
  164.7 102.5 %all-reduce.3.cloned.1.call-start = ((), (), s32[]{:S(2)}) async-start(), calls=%async_computation.4 | async-start | bytes 8388608 | tf_op jit(solution)/shard_map/psum | solution.py:127
  205.7 2.9 %copy-start.12 = (pred[512,768]{1,0:T(32,128)(4,1)S(1)}, pred[512,768]{1,0:T(32,128)(4,1)}, u32[]{:S(2)}) copy-start(pred[512,768]{1,0:T(32,128)(4,1)} %iota_compare_fusion.2) | copy-start | bytes 1179652
  208.6 0.9 copy-start.26
  209.5 1.0 copy-start.10
  209.5 1.7 copy-start.21
  267.2 3.3 %copy-start.11 = (bf16[1,2048,512]{2,1,0:T(8,128)(2,1)S(1)}, bf16[1,2048,512]{2,1,0:T(8,128)(2,1)}, u32[]{:S(2)}) copy-start(bf16[1,2048,512]{2,1,0:T(8,128)(2,1)} %get-tuple-element.47) | copy-start | bytes 6291460
  267.2 4.6 %copy-start.1 = (bf16[1,2048,512]{2,1,0:T(8,128)(2,1)S(1)}, bf16[1,2048,512]{2,1,0:T(8,128)(2,1)}, u32[]{:S(2)}) copy-start(bf16[1,2048,512]{2,1,0:T(8,128)(2,1)} %param.19) | copy-start | bytes 6291460
  (5 other events, 3.6 us)
Sparse Core Ops, SparseCore 0:
  168.6 98.6 all-reduce.2

commit v6 on v4

--- a/solution.py
+++ b/solution.py
@@ -35,7 +35,7 @@
 def expert_forward(flat_in, w_up_one, w_down_one):
     pre_act = jnp.dot(flat_in, w_up_one, preferred_element_type=jnp.float32)
     activated, gelu_slope = gelu_pair(pre_act)
-    hidden = activated.astype(jnp.bfloat16)
+    hidden, gelu_slope = lax.optimization_barrier((activated.astype(jnp.bfloat16), gelu_slope))
     outputs = jnp.dot(hidden, w_down_one, preferred_element_type=jnp.float32).astype(jnp.bfloat16)
     return (hidden, gelu_slope, outputs)
 
@@ -74,9 +74,12 @@
     slot_cot = jnp.concatenate(
         [(gates[:, k:k + 1] * cot_wide).astype(jnp.bfloat16) for k in range(TOP)]
     )
-    flat_hot = route_hot.reshape(-1, n_experts).astype(jnp.int32)
-    before = jnp.cumsum(flat_hot, axis=0, dtype=jnp.int32) - flat_hot
-    slot_rank = jnp.sum(before * flat_hot, axis=1, dtype=jnp.int32).reshape(tok_rows, TOP)
+    flat_hot = jnp.concatenate([routes[:, k:k + 1] == expert_ids[None, :] for k in range(TOP)])
+    order = jnp.arange(TOP * tok_rows, dtype=jnp.int32)
+    earlier = (order[None, :] < order[:, None]).astype(jnp.bfloat16)
+    before = jnp.dot(earlier, flat_hot.astype(jnp.bfloat16), preferred_element_type=jnp.float32)
+    slot_rank = jnp.sum(jnp.where(flat_hot, before, 0.0), axis=1).astype(jnp.int32)
+    slot_rank = slot_rank.reshape(TOP, tok_rows).T
     half = capacity // 2
     rows_in = jnp.concatenate([mixed_in, slot_cot])
     w_up_one = w_up[0]

time: 234 us -> 234 us (level)
  matrix products: 54 us -> 45.9 us
  waiting for transfers between devices: 115 us -> 123 us
  other arithmetic: 10.6 us -> 7.54 us
  local copies, waits for them, and re-layouts: 6.5 us -> 9.3 us
    all_to_all x2, waiting for transfers between devices: 36.2 us -> 44.2 us  [layer_body(): lax.all_to_all(sent.reshape(n_experts, 2 * half, feature_width), 'expert'...]
    dot_general x4, matrix products: 15.3 us -> 10.2 us  [contract_rows(): lax.dot_general(left, right, (((0,), (0,)), ((), ())), preferred_element_...]
    unnamed x35 -> x52, local copies, waits for them, and re-layouts: 5.67 us -> 8.33 us
    dot_general x2, matrix products: 5.87 us -> 8.35 us  [expert_forward(): pre_act = jnp.dot(flat_in, w_up_one, preferred_element_type=jnp.float32)]
  transfers between devices with their start and end apart: 5 -> 5, of which waited for: 5 -> 5; matrix products, arithmetic and copies ran while one was open for 16% -> 12% of each run, Pallas kernels for 0% -> 0%
where the time goes in v6:
time: 234 us; the launch traced here: 233 us
  waiting for transfers between devices  123 us (53%)
  matrix products  45.9 us (20%)
  starting transfers between devices  32.2 us (14%)
  between operations  14.6 us (6%)
  local copies, waits for them, and re-layouts  9.3 us (4%)
  other arithmetic  7.54 us (3%)
    all_to_all x2, waiting for transfers between devices, layer_body(): lax.all_to_all(backs[chunk], 'expert', split_axis=0, concat_axis=0, tiled...  46.6 us
    all_to_all x2, waiting for transfers between devices, layer_body(): lax.all_to_all(sent.reshape(n_experts, 2 * half, feature_width), 'expert'...  44.2 us
    psum x1, waiting for transfers between devices, layer_body(): sum_up = lax.psum(part_up, 'dp')  31.7 us
    all_to_all x2, starting transfers between devices, layer_body(): lax.all_to_all(sent.reshape(n_experts, 2 * half, feature_width), 'expert'...  19.5 us
    all_to_all x2, starting transfers between devices, layer_body(): lax.all_to_all(backs[chunk], 'expert', split_axis=0, concat_axis=0, tiled...  12.6 us
    dot_general x4, matrix products, contract_rows(): lax.dot_general(left, right, (((0,), (0,)), ((), ())), preferred_element_...  10.2 us
    dot_general x4, matrix products, contract_cols(): lax.dot_general(left, right, (((1,), (1,)), ((), ())), preferred_element_...  8.73 us
    dot_general x2, matrix products, expert_forward(): pre_act = jnp.dot(flat_in, w_up_one, preferred_element_type=jnp.float32)  8.35 us
  transfers between devices with their start and end apart: 5, of which 5 were waited for; matrix products, arithmetic and copies ran while one was open for 12% of the time, Pallas kernels for 0%

profile of v6, /device:TPU:1, one launch (start us, length us, event | category | flops | bytes accessed | tf_op | source)
XLA Modules:
  0.0 232.6 jit_solution(9332080884954320605)
XLA Ops:
  10.4 1.2 fusion.105
  11.6 1.4 fusion.75
  13.8 2.0 fusion.48
  15.7 13.1 %all-to-all-start = ((bf16[64,16,512]{2,1,0:T(8,128)(2,1)}), bf16[64,16,512]{2,1,0:T(8,128)(2,1)S(1)}, u32[]{:S(2)}, u32[]{:S(2)}) async-start(bf16[64,16,512]{2,1,0:T(8,128)(2,1)} %bitcast.144), calls=%async_computation | async-start | bytes 2097152 | tf_op jit(solution)/shard_map/all_to_all | solution.py:106
  29.5 3.1 %fusion.45 = bf16[1024,512]{1,0:T(8,128)(2,1)} fusion(pred[1024,512]{1,0:T(32,128)(4,1)S(1)} %iota_compare_fusion.1, pred[1024,256]{1,0:T(32,128)(4,1)S(1)} %fusion.80, bf16[256,512]{1,0:T(8,128)(2,1)} %copy-done.18, bf16[256,512]{1,0:T(8,128)(2,1)} %copy-done.17, bf16[256,512]{1,0:T(8,128)(2,1)} %copy-done.9), kind=kOutput, calls=%fused_computation.57 | convolution fusion | flops 808976384 | bytes 2621440 | tf_op jit(solution)/shard_map/dot_general | solution.py:105
  32.6 24.8 %all-to-all-done = bf16[64,16,512]{2,1,0:T(8,128)(2,1)S(1)} async-done(((bf16[64,16,512]{2,1,0:T(8,128)(2,1)}), bf16[64,16,512]{2,1,0:T(8,128)(2,1)S(1)}, u32[]{:S(2)}, u32[]{:S(2)}) %all-to-all-start) | async-done | bytes 1048608 | tf_op jit(solution)/shard_map/all_to_all | solution.py:106
  57.4 6.4 %all-to-all-start.1 = ((bf16[64,16,512]{2,1,0:T(8,128)(2,1)}), bf16[64,16,512]{2,1,0:T(8,128)(2,1)}, u32[]{:S(2)}, u32[]{:S(2)}) async-start(bf16[64,16,512]{2,1,0:T(8,128)(2,1)} %bitcast.145), calls=%async_computation.1 | async-start | bytes 2097152 | tf_op jit(solution)/shard_map/all_to_all | solution.py:106
  63.8 3.5 %fusion.4 = (f32[512,2048]{1,0:T(8,128)S(1)}, bf16[512,2048]{1,0:T(8,128)(2,1)S(1)}) fusion(bf16[1,512,2048]{2,1,0:T(8,128)(2,1)S(1)} %copy-done, bf16[64,16,512]{2,1,0:T(8,128)(2,1)S(1)} %all-to-all-done), kind=kOutput, calls=%fused_computation.8 | convolution fusion | flops 1093664768 | bytes 8912896 | tf_op jit(solution)/shard_map/dot_general | solution.py:36
  67.4 1.3 multiply_convert_fusion.2
  68.7 2.1 fusion.72
  70.8 2.0 fusion.66
  72.8 19.4 %all-to-all-done.1 = bf16[64,16,512]{2,1,0:T(8,128)(2,1)} async-done(((bf16[64,16,512]{2,1,0:T(8,128)(2,1)}), bf16[64,16,512]{2,1,0:T(8,128)(2,1)}, u32[]{:S(2)}, u32[]{:S(2)}) %all-to-all-start.1) | async-done | bytes 1048608 | tf_op jit(solution)/shard_map/all_to_all | solution.py:106
  92.2 4.8 %fusion.9 = (f32[512,2048]{1,0:T(8,128)S(1)}, bf16[512,2048]{1,0:T(8,128)(2,1)S(1)}) fusion(bf16[1,512,2048]{2,1,0:T(8,128)(2,1)S(1)} %copy-done, bf16[64,16,512]{2,1,0:T(8,128)(2,1)} %all-to-all-done.1), kind=kOutput, calls=%fused_computation.13 | convolution fusion | flops 1093664768 | bytes 8912896 | tf_op jit(solution)/shard_map/dot_general | solution.py:36
  97.1 1.2 pad_maximum_fusion
  98.4 1.5 copy-done.5
  99.8 1.3 fusion.82
  101.4 1.3 fusion.83
  103.0 2.3 multiply_convert_fusion
  105.4 4.0 %fusion.26 = bf16[1,512,2048]{2,1,0:T(8,128)(2,1)} fusion(f32[512,2048]{1,0:T(8,128)S(1)} %fusion.82, bf16[512,2048]{1,0:T(8,128)(2,1)S(1)} %multiply_convert_fusion, bf16[64,16,512]{2,1,0:T(8,128)(2,1)} %all-to-all-done.1), kind=kOutput, calls=%fused_computation.36 | convolution fusion | flops 1075838976 | bytes 8912896 | tf_op jit(solution)/shard_map/dot_general | solution.py:24
  109.4 3.6 %fusion.27 = bf16[1,2048,512]{2,1,0:T(8,128)(2,1)} fusion(f32[2048,512]{1,0:T(8,128)S(1)} %fusion.83, bf16[512,2048]{1,0:T(8,128)(2,1)S(1)} %get-tuple-element.14, bf16[64,16,512]{2,1,0:T(8,128)(2,1)} %all-to-all-done.1), kind=kOutput, calls=%fused_computation.37 | convolution fusion | flops 1075838976 | bytes 8912896 | tf_op jit(solution)/shard_map/dot_general | solution.py:24
  113.0 6.2 %all-to-all-start.2 = ((bf16[64,16,512]{2,1,0:T(8,128)(2,1)}), bf16[64,16,512]{2,1,0:T(8,128)(2,1)S(1)}, u32[]{:S(2)}, u32[]{:S(2)}) async-start(bf16[64,16,512]{2,1,0:T(8,128)(2,1)} %pad_maximum_fusion), calls=%async_computation.2 | async-start | bytes 2097152 | tf_op jit(solution)/shard_map/all_to_all | solution.py:130
  120.0 3.0 %fusion.69 = bf16[64,8,512]{2,1,0:T(8,128)(2,1)S(1)} fusion(bf16[512,2048]{1,0:T(8,128)(2,1)} %copy-done.11, bf16[1,512,2048]{2,1,0:T(8,128)(2,1)S(1)} %copy-done), kind=kOutput, calls=%fused_computation.65 | convolution fusion | flops 1074003968 | bytes 4718592 | tf_op jit(solution)/shard_map/dot_general | solution.py:30
  123.0 1.2 fusion.63
  125.4 22.3 %all-to-all-done.2 = bf16[64,16,512]{2,1,0:T(8,128)(2,1)S(1)} async-done(((bf16[64,16,512]{2,1,0:T(8,128)(2,1)}), bf16[64,16,512]{2,1,0:T(8,128)(2,1)S(1)}, u32[]{:S(2)}, u32[]{:S(2)}) %all-to-all-start.2) | async-done | bytes 1048608 | tf_op jit(solution)/shard_map/all_to_all | solution.py:130
  148.7 6.4 %all-to-all-start.3 = ((bf16[64,16,512]{2,1,0:T(8,128)(2,1)}), bf16[64,16,512]{2,1,0:T(8,128)(2,1)}, u32[]{:S(2)}, u32[]{:S(2)}) async-start(bf16[64,16,512]{2,1,0:T(8,128)(2,1)} %pad_maximum_fusion.1), calls=%async_computation.3 | async-start | bytes 2097152 | tf_op jit(solution)/shard_map/all_to_all | solution.py:130
  157.2 2.1 fusion.10
  159.4 24.2 %all-to-all-done.3 = bf16[64,16,512]{2,1,0:T(8,128)(2,1)} async-done(((bf16[64,16,512]{2,1,0:T(8,128)(2,1)}), bf16[64,16,512]{2,1,0:T(8,128)(2,1)}, u32[]{:S(2)}, u32[]{:S(2)}) %all-to-all-start.3) | async-done | bytes 1048608 | tf_op jit(solution)/shard_map/all_to_all | solution.py:130
  183.6 3.1 %fusion.42 = f32[768,512]{1,0:T(8,128)S(1)} fusion(f32[768,512]{1,0:T(8,128)} %fusion.10, bf16[1024,512]{1,0:T(8,128)(2,1)} %bitcast.32, pred[256,1024]{1,0:T(32,128)(4,1)} %fusion.81, pred[512,1024]{1,0:T(32,128)(4,1)S(1)} %iota_compare_fusion), kind=kOutput, calls=%fused_computation.56 | convolution fusion | flops 806486016 | bytes 4980736 | tf_op jit(solution)/shard_map/dot_general | solution.py:138
  188.4 1.1 fusion.76
  189.5 31.7 %all-reduce.3.cloned.1.call-done = (bf16[1,512,2048]{2,1,0:T(8,128)(2,1)}, bf16[1,2048,512]{2,1,0:T(8,128)(2,1)}) async-done(((bf16[1,512,2048]{2,1,0:T(8,128)(2,1)}, bf16[1,2048,512]{2,1,0:T(8,128)(2,1)}), (bf16[1,512,2048]{2,1,0:T(8,128)(2,1)}, bf16[1,2048,512]{2,1,0:T(8,128)(2,1)})) %all-reduce.3.cloned.1.call-update) | async-done | bytes 4194320 | tf_op jit(solution)/shard_map/psum | solution.py:125
  221.2 3.3 %copy.51 = bf16[1,512,2048]{2,1,0:T(8,128)(2,1)} copy(bf16[1,512,2048]{2,1,0:T(8,128)(2,1)} %get-tuple-element.54) | data formatting | bytes 4194304
  224.5 1.3 copy.52
  (85 shorter events, 11.6 us)
Async XLA Ops:
  7.2 56.6 %copy-start = (bf16[1,512,2048]{2,1,0:T(8,128)(2,1)S(1)}, bf16[1,512,2048]{2,1,0:T(8,128)(2,1)}, u32[]{:S(2)}) copy-start(bf16[1,512,2048]{2,1,0:T(8,128)(2,1)} %param.18) | copy-start | bytes 6291460
  7.2 6.1 %copy-start.20 = (s32[256,2]{0,1:T(2,128)S(1)}, s32[256,2]{0,1:T(2,128)}, u32[]{:S(2)}) copy-start(s32[256,2]{0,1:T(2,128)} %param.12) | copy-start | bytes 6148
  7.2 5.8 %copy-start.19 = (bf16[512,64]{0,1:T(8,128)(2,1)S(1)}, bf16[512,64]{0,1:T(8,128)(2,1)}, u32[]{:S(2)}) copy-start(bf16[512,64]{0,1:T(8,128)(2,1)} %param.17) | copy-start | bytes 196612
  7.2 6.4 %copy-start.8 = (bf16[256,512]{1,0:T(8,128)(2,1)S(1)}, bf16[256,512]{1,0:T(8,128)(2,1)}, u32[]{:S(2)}) copy-start(bf16[256,512]{1,0:T(8,128)(2,1)} %param.13) | copy-start | bytes 786436
  13.0 2.7 %copy-start.9 = (bf16[256,512]{1,0:T(8,128)(2,1)}, bf16[256,512]{1,0:T(8,128)(2,1)S(1)}, u32[]{:S(2)}) copy-start(bf16[256,512]{1,0:T(8,128)(2,1)S(1)} %fusion.75) | copy-start | bytes 786436
  13.7 2.0 copy-start.17
  13.7 2.0 copy-start.18
  15.7 41.7 %all-to-all-start = ((bf16[64,16,512]{2,1,0:T(8,128)(2,1)}), bf16[64,16,512]{2,1,0:T(8,128)(2,1)S(1)}, u32[]{:S(2)}, u32[]{:S(2)}) async-start(bf16[64,16,512]{2,1,0:T(8,128)(2,1)} %bitcast.144), calls=%async_computation | async-start | bytes 2097152 | tf_op jit(solution)/shard_map/all_to_all | solution.py:106
  57.4 34.8 %all-to-all-start.1 = ((bf16[64,16,512]{2,1,0:T(8,128)(2,1)}), bf16[64,16,512]{2,1,0:T(8,128)(2,1)}, u32[]{:S(2)}, u32[]{:S(2)}) async-start(bf16[64,16,512]{2,1,0:T(8,128)(2,1)} %bitcast.145), calls=%async_computation.1 | async-start | bytes 2097152 | tf_op jit(solution)/shard_map/all_to_all | solution.py:106
  63.8 3.6 %copy-start.1 = (bf16[1,2048,512]{2,1,0:T(8,128)(2,1)S(1)}, bf16[1,2048,512]{2,1,0:T(8,128)(2,1)}, u32[]{:S(2)}) copy-start(bf16[1,2048,512]{2,1,0:T(8,128)(2,1)} %param.19) | copy-start | bytes 6291460
  67.4 3.4 %copy-start.6 = (bf16[512,2048]{1,0:T(8,128)(2,1)}, bf16[512,2048]{1,0:T(8,128)(2,1)S(1)}, u32[]{:S(2)}) copy-start(bf16[512,2048]{1,0:T(8,128)(2,1)S(1)} %get-tuple-element.11) | copy-start | bytes 6291460
  68.7 2.1 copy-start.4
  92.2 4.9 %copy-start.15 = (bf16[64,8,512]{2,1,0:T(8,128)(2,1)S(1)}, bf16[64,8,512]{2,1,0:T(8,128)(2,1)}, u32[]{:S(2)}) copy-start(bf16[64,8,512]{2,1,0:T(8,128)(2,1)} %fusion.72) | copy-start | bytes 1572868
  92.2 4.9 %copy-start.16 = (bf16[64,8,512]{2,1,0:T(8,128)(2,1)S(1)}, bf16[64,8,512]{2,1,0:T(8,128)(2,1)}, u32[]{:S(2)}) copy-start(bf16[64,8,512]{2,1,0:T(8,128)(2,1)} %fusion.66) | copy-start | bytes 1572868
  97.1 12.3 %copy-start.21 = (bf16[512,2048]{1,0:T(8,128)(2,1)}, bf16[512,2048]{1,0:T(8,128)(2,1)S(1)}, u32[]{:S(2)}) copy-start(bf16[512,2048]{1,0:T(8,128)(2,1)S(1)} %get-tuple-element.14) | copy-start | bytes 6291460
  97.1 2.7 %copy-start.5 = (bf16[512,2048]{1,0:T(8,128)(2,1)S(1)}, bf16[512,2048]{1,0:T(8,128)(2,1)}, u32[]{:S(2)}) copy-start(bf16[512,2048]{1,0:T(8,128)(2,1)} %copy-done.4) | copy-start | bytes 6291460
  99.8 1.6 copy-start.7
  101.4 1.6 copy-start.2
  105.3 4.1 %copy-start.11 = (bf16[512,2048]{1,0:T(8,128)(2,1)}, bf16[512,2048]{1,0:T(8,128)(2,1)S(1)}, u32[]{:S(2)}) copy-start(bf16[512,2048]{1,0:T(8,128)(2,1)S(1)} %multiply_convert_fusion) | copy-start | bytes 6291460
  113.0 34.7 %all-to-all-start.2 = ((bf16[64,16,512]{2,1,0:T(8,128)(2,1)}), bf16[64,16,512]{2,1,0:T(8,128)(2,1)S(1)}, u32[]{:S(2)}, u32[]{:S(2)}) async-start(bf16[64,16,512]{2,1,0:T(8,128)(2,1)} %pad_maximum_fusion), calls=%async_computation.2 | async-start | bytes 2097152 | tf_op jit(solution)/shard_map/all_to_all | solution.py:130
  119.2 101.9 %all-reduce.3.cloned.1.call-start = ((), (), s32[]{:S(2)}) async-start(), calls=%async_computation.4 | async-start | bytes 8388608 | tf_op jit(solution)/shard_map/psum | solution.py:125
  120.0 3.1 %copy-start.3 = (bf16[1,2048,512]{2,1,0:T(8,128)(2,1)S(1)}, bf16[1,2048,512]{2,1,0:T(8,128)(2,1)}, u32[]{:S(2)}) copy-start(bf16[1,2048,512]{2,1,0:T(8,128)(2,1)} %param.19) | copy-start | bytes 6291460
  120.0 3.1 %copy-start.22 = (bf16[512,2048]{1,0:T(8,128)(2,1)S(1)}, bf16[512,2048]{1,0:T(8,128)(2,1)}, u32[]{:S(2)}) copy-start(bf16[512,2048]{1,0:T(8,128)(2,1)} %copy-done.21) | copy-start | bytes 6291460
  147.8 1.0 copy-start.13
  148.7 34.8 %all-to-all-start.3 = ((bf16[64,16,512]{2,1,0:T(8,128)(2,1)}), bf16[64,16,512]{2,1,0:T(8,128)(2,1)}, u32[]{:S(2)}, u32[]{:S(2)}) async-start(bf16[64,16,512]{2,1,0:T(8,128)(2,1)} %pad_maximum_fusion.1), calls=%async_computation.3 | async-start | bytes 2097152 | tf_op jit(solution)/shard_map/all_to_all | solution.py:130
  155.1 2.1 copy-start.14
  186.6 1.0 copy-start.10
  221.2 3.3 %copy-start.12 = (bf16[1,2048,512]{2,1,0:T(8,128)(2,1)S(1)}, bf16[1,2048,512]{2,1,0:T(8,128)(2,1)}, u32[]{:S(2)}) copy-start(bf16[1,2048,512]{2,1,0:T(8,128)(2,1)} %get-tuple-element.55) | copy-start | bytes 6291460
Sparse Core Ops, SparseCore 0:
  122.5 98.6 all-reduce.2

commit v7 on v6

--- a/solution.py
+++ b/solution.py
@@ -35,7 +35,7 @@
 def expert_forward(flat_in, w_up_one, w_down_one):
     pre_act = jnp.dot(flat_in, w_up_one, preferred_element_type=jnp.float32)
     activated, gelu_slope = gelu_pair(pre_act)
-    hidden, gelu_slope = lax.optimization_barrier((activated.astype(jnp.bfloat16), gelu_slope))
+    hidden = activated.astype(jnp.bfloat16)
     outputs = jnp.dot(hidden, w_down_one, preferred_element_type=jnp.float32).astype(jnp.bfloat16)
     return (hidden, gelu_slope, outputs)
 
@@ -58,10 +58,7 @@
     capacity = 2 * TOP * tok_rows // n_experts
     pos_hidden = jax.nn.relu(jnp.dot(pos_table, tower_in, preferred_element_type=jnp.float32))
     pos_rows = jnp.dot(pos_hidden, tower_out.astype(jnp.float32), precision=lax.Precision.HIGHEST)
-    slot_hot = (slots[:, None] == jnp.arange(pos_table.shape[0], dtype=jnp.int32)[None, :]).astype(
-        jnp.float32
-    )
-    pos_feats = jnp.dot(slot_hot, pos_rows, precision=lax.Precision.HIGHEST)
+    pos_feats = jnp.take(pos_rows, slots, axis=0)
     mixed_in = (features.astype(jnp.float32) + pos_feats).astype(jnp.bfloat16)
     logits = jnp.dot(mixed_in, router, preferred_element_type=jnp.float32)
     expert_ids = jnp.arange(n_experts, dtype=jnp.int32)

time: 234 us -> 235 us (level)
  waiting for transfers between devices: 123 us -> 112 us
  matrix products: 45.9 us -> 52.8 us
  local copies, waits for them, and re-layouts: 9.3 us -> 13.2 us
    all_to_all x2, waiting for transfers between devices: 44.2 us -> 36.1 us  [layer_body(): lax.all_to_all(sent.reshape(n_experts, 2 * half, feature_width), 'expert'...]
    dot_general x4, matrix products: 10.2 us -> 15.3 us  [contract_rows(): lax.dot_general(left, right, (((0,), (0,)), ((), ())), preferred_element_...]
    unnamed x52 -> x44, local copies, waits for them, and re-layouts: 8.33 us -> 11.2 us
    dot_general x2, matrix products: 8.35 us -> 5.87 us  [expert_forward(): pre_act = jnp.dot(flat_in, w_up_one, preferred_element_type=jnp.float32)]
  transfers between devices with their start and end apart: 5 -> 5, of which waited for: 5 -> 5; matrix products, arithmetic and copies ran while one was open for 12% -> 17% of each run, Pallas kernels for 0% -> 0%
where the time goes in v7:
time: 235 us; the launch traced here: 234 us
  waiting for transfers between devices  112 us (48%)
  matrix products  52.8 us (22%)
  starting transfers between devices  32.2 us (14%)
  between operations  14.6 us (6%)
  local copies, waits for them, and re-layouts  13.2 us (6%)
  other arithmetic  9.19 us (4%)
    all_to_all x2, waiting for transfers between devices, layer_body(): lax.all_to_all(backs[chunk], 'expert', split_axis=0, concat_axis=0, tiled...  44.5 us
    all_to_all x2, waiting for transfers between devices, layer_body(): lax.all_to_all(sent.reshape(n_experts, 2 * half, feature_width), 'expert'...  36.1 us
    psum x1, waiting for transfers between devices, layer_body(): sum_up = lax.psum(part_up, 'dp')  30.5 us
    all_to_all x2, starting transfers between devices, layer_body(): lax.all_to_all(sent.reshape(n_experts, 2 * half, feature_width), 'expert'...  19.6 us
    dot_general x4, matrix products, contract_rows(): lax.dot_general(left, right, (((0,), (0,)), ((), ())), preferred_element_...  15.3 us
    all_to_all x2, starting transfers between devices, layer_body(): lax.all_to_all(backs[chunk], 'expert', split_axis=0, concat_axis=0, tiled...  12.6 us
    unnamed x44, local copies, waits for them, and re-layouts  11.2 us
    dot_general x4, matrix products, contract_cols(): lax.dot_general(left, right, (((1,), (1,)), ((), ())), preferred_element_...  10.7 us
  transfers between devices with their start and end apart: 5, of which 5 were waited for; matrix products, arithmetic and copies ran while one was open for 17% of the time, Pallas kernels for 0%

profile of v7, /device:TPU:1, one launch (start us, length us, event | category | flops | bytes accessed | tf_op | source)
XLA Modules:
  0.0 233.7 jit_solution(14689323387918639187)
XLA Ops:
  11.7 1.8 copy.23
  14.4 1.2 fusion.107
  18.8 2.0 fusion.52
  20.8 13.2 %all-to-all-start = ((bf16[64,16,512]{2,1,0:T(8,128)(2,1)}), bf16[64,16,512]{2,1,0:T(8,128)(2,1)S(1)}, u32[]{:S(2)}, u32[]{:S(2)}) async-start(bf16[64,16,512]{2,1,0:T(8,128)(2,1)} %bitcast.132), calls=%async_computation | async-start | bytes 2097152 | tf_op jit(solution)/shard_map/all_to_all | solution.py:103
  34.6 3.1 %fusion.49 = bf16[1024,512]{1,0:T(8,128)(2,1)} fusion(pred[1024,512]{1,0:T(32,128)(4,1)S(1)} %iota_compare_fusion.1, pred[1024,256]{1,0:T(32,128)(4,1)S(1)} %fusion.83, bf16[256,512]{0,1:T(8,128)(2,1)} %copy-done.11, bf16[256,512]{0,1:T(8,128)(2,1)} %copy-done.10, bf16[256,512]{0,1:T(8,128)(2,1)} %copy-done.5), kind=kOutput, calls=%fused_computation.60 | convolution fusion | flops 808976384 | bytes 2621440 | tf_op jit(solution)/shard_map/dot_general | solution.py:102
  37.7 24.8 %all-to-all-done = bf16[64,16,512]{2,1,0:T(8,128)(2,1)S(1)} async-done(((bf16[64,16,512]{2,1,0:T(8,128)(2,1)}), bf16[64,16,512]{2,1,0:T(8,128)(2,1)S(1)}, u32[]{:S(2)}, u32[]{:S(2)}) %all-to-all-start) | async-done | bytes 1048608 | tf_op jit(solution)/shard_map/all_to_all | solution.py:103
  62.5 6.4 %all-to-all-start.1 = ((bf16[64,16,512]{2,1,0:T(8,128)(2,1)}), bf16[64,16,512]{2,1,0:T(8,128)(2,1)}, u32[]{:S(2)}, u32[]{:S(2)}) async-start(bf16[64,16,512]{2,1,0:T(8,128)(2,1)} %bitcast.131), calls=%async_computation.1 | async-start | bytes 2097152 | tf_op jit(solution)/shard_map/all_to_all | solution.py:103
  68.9 2.8 %fusion.44 = f32[512,2048]{1,0:T(8,128)S(1)} fusion(bf16[1,512,2048]{2,1,0:T(8,128)(2,1)} %param.18, bf16[64,16,512]{2,1,0:T(8,128)(2,1)S(1)} %all-to-all-done), kind=kOutput, calls=%fused_computation.53 | convolution fusion | flops 1073741824 | bytes 6815744 | tf_op jit(solution)/shard_map/dot_general | solution.py:36
  71.7 3.3 %fusion.6 = bf16[512,2048]{1,0:T(8,128)(2,1)S(1)} fusion(f32[512,2048]{1,0:T(8,128)S(1)} %fusion.44, bf16[1,2048,512]{2,1,0:T(8,128)(2,1)S(1)} %copy-done, bf16[64,16,512]{2,1,0:T(8,128)(2,1)S(1)} %all-to-all-done), kind=kOutput, calls=%fused_computation.11 | convolution fusion | flops 1093664768 | bytes 8912896 | tf_op jit(solution)/shard_map/dot_general | solution.py:30
  75.0 1.3 fusion.76
  76.3 1.4 fusion.70
  77.8 1.2 pad_maximum_fusion
  79.0 3.3 %fusion.85 = f32[512,2048]{1,0:T(8,128)} fusion(bf16[512,2048]{1,0:T(8,128)(2,1)S(1)} %fusion.6, bf16[64,16,512]{2,1,0:T(8,128)(2,1)S(1)} %all-to-all-done), kind=kOutput, calls=%fused_computation.105 | convolution fusion | flops 1073741824 | bytes 6815744 | tf_op jit(solution)/shard_map/dot_general | solution.py:24
  82.2 3.8 %fusion.86 = f32[2048,512]{1,0:T(8,128)} fusion(bf16[64,16,512]{2,1,0:T(8,128)(2,1)S(1)} %all-to-all-done, f32[512,2048]{1,0:T(8,128)S(1)} %fusion.44), kind=kOutput, calls=%fused_computation.106 | convolution fusion | flops 1083179008 | bytes 8912896 | tf_op jit(solution)/shard_map/dot_general | solution.py:24
  86.0 11.3 %all-to-all-done.1 = bf16[64,16,512]{2,1,0:T(8,128)(2,1)} async-done(((bf16[64,16,512]{2,1,0:T(8,128)(2,1)}), bf16[64,16,512]{2,1,0:T(8,128)(2,1)}, u32[]{:S(2)}, u32[]{:S(2)}) %all-to-all-start.1) | async-done | bytes 1048608 | tf_op jit(solution)/shard_map/all_to_all | solution.py:103
  97.3 3.0 %fusion.40 = f32[512,2048]{1,0:T(8,128)S(1)} fusion(bf16[1,512,2048]{2,1,0:T(8,128)(2,1)} %param.18, bf16[64,16,512]{2,1,0:T(8,128)(2,1)} %all-to-all-done.1), kind=kOutput, calls=%fused_computation.49 | convolution fusion | flops 1073741824 | bytes 6815744 | tf_op jit(solution)/shard_map/dot_general | solution.py:36
  100.3 4.9 %fusion.13 = bf16[512,2048]{1,0:T(8,128)(2,1)S(1)} fusion(f32[512,2048]{1,0:T(8,128)S(1)} %fusion.40, bf16[1,2048,512]{2,1,0:T(8,128)(2,1)S(1)} %copy-done, bf16[64,16,512]{2,1,0:T(8,128)(2,1)} %all-to-all-done.1), kind=kOutput, calls=%fused_computation.18 | convolution fusion | flops 1093664768 | bytes 8912896 | tf_op jit(solution)/shard_map/dot_general | solution.py:30
  105.3 4.6 %fusion.31 = bf16[1,2048,512]{2,1,0:T(8,128)(2,1)} fusion(f32[2048,512]{1,0:T(8,128)S(1)} %copy-done.16, bf16[64,16,512]{2,1,0:T(8,128)(2,1)} %all-to-all-done.1, f32[512,2048]{1,0:T(8,128)S(1)} %fusion.40), kind=kOutput, calls=%fused_computation.40 | convolution fusion | flops 1085276160 | bytes 11010048 | tf_op jit(solution)/shard_map/dot_general | solution.py:24
  109.9 3.6 %fusion.30 = bf16[1,512,2048]{2,1,0:T(8,128)(2,1)} fusion(f32[512,2048]{1,0:T(8,128)S(1)} %copy-done.4, bf16[512,2048]{1,0:T(8,128)(2,1)S(1)} %fusion.13, bf16[64,16,512]{2,1,0:T(8,128)(2,1)} %all-to-all-done.1), kind=kOutput, calls=%fused_computation.39 | convolution fusion | flops 1075838976 | bytes 8912896 | tf_op jit(solution)/shard_map/dot_general | solution.py:24
  113.5 6.2 %all-to-all-start.2 = ((bf16[64,16,512]{2,1,0:T(8,128)(2,1)}), bf16[64,16,512]{2,1,0:T(8,128)(2,1)S(1)}, u32[]{:S(2)}, u32[]{:S(2)}) async-start(bf16[64,16,512]{2,1,0:T(8,128)(2,1)} %pad_maximum_fusion), calls=%async_computation.2 | async-start | bytes 2097152 | tf_op jit(solution)/shard_map/all_to_all | solution.py:127
  120.5 3.8 %fusion.67 = bf16[64,8,512]{2,1,0:T(8,128)(2,1)S(1)} fusion(bf16[1,2048,512]{2,1,0:T(8,128)(2,1)S(1)} %copy-done, f32[512,2048]{1,0:T(8,128)} %copy-done.3), kind=kOutput, calls=%fused_computation.66 | convolution fusion | flops 1083441152 | bytes 6815744 | tf_op jit(solution)/shard_map/dot_general | solution.py:39
  124.3 1.3 fusion.73
  125.6 1.1 pad_maximum_fusion.1
  126.7 21.5 %all-to-all-done.2 = bf16[64,16,512]{2,1,0:T(8,128)(2,1)S(1)} async-done(((bf16[64,16,512]{2,1,0:T(8,128)(2,1)}), bf16[64,16,512]{2,1,0:T(8,128)(2,1)S(1)}, u32[]{:S(2)}, u32[]{:S(2)}) %all-to-all-start.2) | async-done | bytes 1048608 | tf_op jit(solution)/shard_map/all_to_all | solution.py:127
  149.2 6.4 %all-to-all-start.3 = ((bf16[64,16,512]{2,1,0:T(8,128)(2,1)}), bf16[64,16,512]{2,1,0:T(8,128)(2,1)}, u32[]{:S(2)}, u32[]{:S(2)}) async-start(bf16[64,16,512]{2,1,0:T(8,128)(2,1)} %pad_maximum_fusion.1), calls=%async_computation.3 | async-start | bytes 2097152 | tf_op jit(solution)/shard_map/all_to_all | solution.py:127
  157.7 3.4 %fusion.14 = f32[768,512]{0,1:T(8,128)} fusion(bf16[1024,512]{1,0:T(8,128)(2,1)} %bitcast.130, pred[256,1024]{1,0:T(32,128)(4,1)S(1)} %fusion.81, pred[512,1024]{1,0:T(32,128)(4,1)S(1)} %iota_compare_fusion.3), kind=kOutput, calls=%fused_computation.23 | convolution fusion | flops 806092800 | bytes 3407872 | tf_op jit(solution)/shard_map/dot_general | solution.py:135
  161.1 23.0 %all-to-all-done.3 = bf16[64,16,512]{2,1,0:T(8,128)(2,1)} async-done(((bf16[64,16,512]{2,1,0:T(8,128)(2,1)}), bf16[64,16,512]{2,1,0:T(8,128)(2,1)}, u32[]{:S(2)}, u32[]{:S(2)}) %all-to-all-start.3) | async-done | bytes 1048608 | tf_op jit(solution)/shard_map/all_to_all | solution.py:127
  184.1 3.1 %fusion.46 = f32[768,512]{0,1:T(8,128)S(1)} fusion(f32[768,512]{0,1:T(8,128)} %fusion.14, bf16[1024,512]{1,0:T(8,128)(2,1)} %bitcast.32, pred[256,1024]{1,0:T(32,128)(4,1)} %fusion.84, pred[512,1024]{1,0:T(32,128)(4,1)S(1)} %iota_compare_fusion), kind=kOutput, calls=%fused_computation.59 | convolution fusion | flops 806486016 | bytes 4980736 | tf_op jit(solution)/shard_map/dot_general | solution.py:135
  189.4 1.5 fusion.79
  191.7 30.5 %all-reduce.3.cloned.1.call-done = (bf16[1,512,2048]{2,1,0:T(8,128)(2,1)}, bf16[1,2048,512]{2,1,0:T(8,128)(2,1)}) async-done(((bf16[1,512,2048]{2,1,0:T(8,128)(2,1)}, bf16[1,2048,512]{2,1,0:T(8,128)(2,1)}), (bf16[1,512,2048]{2,1,0:T(8,128)(2,1)}, bf16[1,2048,512]{2,1,0:T(8,128)(2,1)})) %all-reduce.3.cloned.1.call-update) | async-done | bytes 4194320 | tf_op jit(solution)/shard_map/psum | solution.py:122
  222.2 3.3 %copy.58 = bf16[1,512,2048]{2,1,0:T(8,128)(2,1)} copy(bf16[1,512,2048]{2,1,0:T(8,128)(2,1)} %get-tuple-element.50) | data formatting | bytes 4194304
  225.5 1.3 copy.59
  (82 shorter events, 15.7 us)
Async XLA Ops:
  7.2 64.6 %copy-start = (bf16[1,2048,512]{2,1,0:T(8,128)(2,1)S(1)}, bf16[1,2048,512]{2,1,0:T(8,128)(2,1)}, u32[]{:S(2)}) copy-start(bf16[1,2048,512]{2,1,0:T(8,128)(2,1)} %param.19) | copy-start | bytes 6291460
  9.8 8.0 %copy-start.12 = (bf16[512,64]{0,1:T(8,128)(2,1)S(1)}, bf16[512,64]{0,1:T(8,128)(2,1)}, u32[]{:S(2)}) copy-start(bf16[512,64]{0,1:T(8,128)(2,1)} %param.17) | copy-start | bytes 196612
  11.7 6.3 %copy-start.13 = (s32[256,2]{0,1:T(2,128)S(1)}, s32[256,2]{0,1:T(2,128)}, u32[]{:S(2)}) copy-start(s32[256,2]{0,1:T(2,128)} %param.12) | copy-start | bytes 6148
  17.8 3.0 %copy-start.5 = (bf16[256,512]{0,1:T(8,128)(2,1)}, bf16[256,512]{0,1:T(8,128)(2,1)S(1)}, u32[]{:S(2)}) copy-start(bf16[256,512]{0,1:T(8,128)(2,1)S(1)} %add_convert_fusion.3) | copy-start | bytes 786436
  18.8 2.0 copy-start.10
  18.8 2.0 copy-start.11
  20.8 41.7 %all-to-all-start = ((bf16[64,16,512]{2,1,0:T(8,128)(2,1)}), bf16[64,16,512]{2,1,0:T(8,128)(2,1)S(1)}, u32[]{:S(2)}, u32[]{:S(2)}) async-start(bf16[64,16,512]{2,1,0:T(8,128)(2,1)} %bitcast.132), calls=%async_computation | async-start | bytes 2097152 | tf_op jit(solution)/shard_map/all_to_all | solution.py:103
  62.5 34.8 %all-to-all-start.1 = ((bf16[64,16,512]{2,1,0:T(8,128)(2,1)}), bf16[64,16,512]{2,1,0:T(8,128)(2,1)}, u32[]{:S(2)}, u32[]{:S(2)}) async-start(bf16[64,16,512]{2,1,0:T(8,128)(2,1)} %bitcast.131), calls=%async_computation.1 | async-start | bytes 2097152 | tf_op jit(solution)/shard_map/all_to_all | solution.py:103
  71.7 3.3 %copy-start.1 = (bf16[1,512,2048]{2,1,0:T(8,128)(2,1)S(1)}, bf16[1,512,2048]{2,1,0:T(8,128)(2,1)}, u32[]{:S(2)}) copy-start(bf16[1,512,2048]{2,1,0:T(8,128)(2,1)} %param.18) | copy-start | bytes 6291460
  100.3 4.9 %copy-start.3 = (f32[512,2048]{1,0:T(8,128)}, f32[512,2048]{1,0:T(8,128)S(1)}, u32[]{:S(2)}) copy-start(f32[512,2048]{1,0:T(8,128)S(1)} %fusion.40) | copy-start | bytes 12582916
  100.3 4.9 %copy-start.16 = (f32[2048,512]{1,0:T(8,128)S(1)}, f32[2048,512]{1,0:T(8,128)}, u32[]{:S(2)}) copy-start(f32[2048,512]{1,0:T(8,128)} %fusion.86) | copy-start | bytes 12582916
  105.2 4.6 %copy-start.14 = (bf16[512,2048]{1,0:T(8,128)(2,1)}, bf16[512,2048]{1,0:T(8,128)(2,1)S(1)}, u32[]{:S(2)}) copy-start(bf16[512,2048]{1,0:T(8,128)(2,1)S(1)} %fusion.13) | copy-start | bytes 6291460
  105.3 4.6 %copy-start.4 = (f32[512,2048]{1,0:T(8,128)S(1)}, f32[512,2048]{1,0:T(8,128)}, u32[]{:S(2)}) copy-start(f32[512,2048]{1,0:T(8,128)} %fusion.85) | copy-start | bytes 12582916
  113.5 34.7 %all-to-all-start.2 = ((bf16[64,16,512]{2,1,0:T(8,128)(2,1)}), bf16[64,16,512]{2,1,0:T(8,128)(2,1)S(1)}, u32[]{:S(2)}, u32[]{:S(2)}) async-start(bf16[64,16,512]{2,1,0:T(8,128)(2,1)} %pad_maximum_fusion), calls=%async_computation.2 | async-start | bytes 2097152 | tf_op jit(solution)/shard_map/all_to_all | solution.py:127
  119.7 102.5 %all-reduce.3.cloned.1.call-start = ((), (), s32[]{:S(2)}) async-start(), calls=%async_computation.4 | async-start | bytes 8388608 | tf_op jit(solution)/shard_map/psum | solution.py:122
  120.5 3.8 %copy-start.2 = (bf16[1,512,2048]{2,1,0:T(8,128)(2,1)S(1)}, bf16[1,512,2048]{2,1,0:T(8,128)(2,1)}, u32[]{:S(2)}) copy-start(bf16[1,512,2048]{2,1,0:T(8,128)(2,1)} %param.18) | copy-start | bytes 6291460
  120.5 3.8 %copy-start.15 = (bf16[512,2048]{1,0:T(8,128)(2,1)S(1)}, bf16[512,2048]{1,0:T(8,128)(2,1)}, u32[]{:S(2)}) copy-start(bf16[512,2048]{1,0:T(8,128)(2,1)} %copy-done.14) | copy-start | bytes 6291460
  148.2 1.0 copy-start.9
  149.2 34.8 %all-to-all-start.3 = ((bf16[64,16,512]{2,1,0:T(8,128)(2,1)}), bf16[64,16,512]{2,1,0:T(8,128)(2,1)}, u32[]{:S(2)}, u32[]{:S(2)}) async-start(bf16[64,16,512]{2,1,0:T(8,128)(2,1)} %pad_maximum_fusion.1), calls=%async_computation.3 | async-start | bytes 2097152 | tf_op jit(solution)/shard_map/all_to_all | solution.py:127
  184.1 4.3 %copy-start.6 = (bf16[256,512]{0,1:T(8,128)(2,1)S(1)}, bf16[256,512]{0,1:T(8,128)(2,1)}, u32[]{:S(2)}) copy-start(bf16[256,512]{0,1:T(8,128)(2,1)} %copy-done.5) | copy-start | bytes 786436
  187.2 1.1 copy-start.8
  222.2 3.3 %copy-start.7 = (bf16[1,2048,512]{2,1,0:T(8,128)(2,1)S(1)}, bf16[1,2048,512]{2,1,0:T(8,128)(2,1)}, u32[]{:S(2)}) copy-start(bf16[1,2048,512]{2,1,0:T(8,128)(2,1)} %get-tuple-element.51) | copy-start | bytes 6291460
Sparse Core Ops, SparseCore 0:
  123.5 98.6 all-reduce.2
